TPU v7x, 512 devices: a whole 4x8x8 slice. The times are simulated.
512 devices in a mesh: head: 8 (over z), ctx: 64 (over x, y, core).
Axes of the slice: x: 4, y: 8, z: 8, core: 2. Of those that a mesh axis runs over, the one named last changes fastest.
Arguments:
- query_bits: int32 [256, 16384], P('head', 'ctx'), may hold values from 0 to 65535
- key_bits: int32 [256, 16384], P('head', 'ctx'), may hold values from 0 to 65535
- values: bfloat16 [16384, 4096], P('ctx', 'head'), may hold values from -6 to 6
- grad_out: bfloat16 [64, 256, 4096], P('ctx', 'head'), may hold values from -6 to 6
- tile_mask: int32 [64, 2, 2], P('ctx'), may hold values 0 or 1
Outputs:
- query_grad: bfloat16 [16384, 4096], P('ctx', 'head')
- key_grad: bfloat16 [16384, 4096], P('ctx', 'head')
- value_grad: bfloat16 [16384, 4096], P('ctx', 'head')
All inputs are finite; a program needn't handle non-finite values. No bound on the sum of `tile_mask` on one device may be relied on, other than what follows from the above.
Results may differ from a plain program's by a relative error of at most 0.0049.
Values may be sent and summed in bfloat16 or wider, within the bound.
No kernel may reach another device: no remote copies, remote signals or barrier semaphores. Data moves between devices by JAX's collectives and lax.ppermute only.
A program may use at most 128 MiB of HBM per device.

v0:
```python
import math

import jax
import jax.numpy as jnp
import numpy as np
from jax import lax
from jax.sharding import Mesh
from jax.sharding import PartitionSpec as P

HD = 128
CTX = ("x", "y", "core")

def unpack_bits(packed, heads_here):
    shifts = jnp.arange(16, dtype=jnp.int32).reshape(1, 1, 16, 1)
    spread = jnp.right_shift(packed.reshape(heads_here, -1, 1, packed.shape[-1]), shifts)
    return jnp.bitwise_and(spread, 1).astype(jnp.bfloat16).reshape(heads_here, -1, packed.shape[-1])


def token_mask(tiles, tile_size):
    tile_count = tiles.shape[0]
    tile_index = jnp.arange(tile_count, dtype=jnp.int32)
    lower = tile_index[:, None] > tile_index[None, :]
    diagonal = tile_index[:, None] == tile_index[None, :]
    allowed = jnp.where(diagonal, 1.0, jnp.where(lower, tiles.astype(jnp.float32), 0.0))
    span_width = tile_count * tile_size
    expanded = jnp.broadcast_to(
        allowed[:, None, :, None], (tile_count, tile_size, tile_count, tile_size)
    ).reshape(span_width, span_width)
    position = jnp.arange(span_width, dtype=jnp.int32)
    return jnp.where(position[:, None] >= position[None, :], expanded, 0.0)


def gather_heads(grad_out, n_head, width):
    tok_part = grad_out.shape[1]
    blocks = grad_out[0].reshape(tok_part, n_head, width).transpose(1, 0, 2)
    got = lax.all_to_all(blocks, "head", 0, 0, tiled=True)
    return got.reshape(n_head * tok_part, width)


def carried_sums(state_term, adj_term, n_ctx):
    f32 = jnp.float32
    heads = state_term.shape[0]
    terms = jnp.concatenate([state_term, adj_term], axis=0).reshape(n_ctx, -1, HD)
    got = lax.all_to_all(terms, CTX, 0, 0, tiled=True)
    me = lax.axis_index(CTX)
    row = jnp.arange(n_ctx, dtype=jnp.int32)[:, None]
    col = jnp.arange(n_ctx, dtype=jnp.int32)[None, :]
    mix = jnp.where(me < n_ctx // 2, col < row, col > row).astype(f32)
    sums = jnp.dot(
        mix, got.reshape(n_ctx, -1), precision=lax.Precision.HIGHEST, preferred_element_type=f32
    )
    back = lax.all_to_all(sums.astype(jnp.bfloat16).reshape(n_ctx, -1, HD), CTX, 0, 0, tiled=True)
    both = back.reshape(2, heads, HD, HD)
    return both[0], both[1]


def make_local(sizes, n_head):
    n_ctx = sizes[0] * sizes[1] * sizes[2]

    def local(query_bits, key_bits, values, grad_out, tile_mask):
        f32 = jnp.float32
        bf16 = jnp.bfloat16
        tok_rows = values.shape[0]
        head_group = values.shape[1] // HD
        att_scale = 4.0 / (HD * math.sqrt(tok_rows * n_ctx))
        q = unpack_bits(query_bits, head_group)
        k = unpack_bits(key_bits, head_group)
        v = values.reshape(tok_rows, head_group, HD)
        g = gather_heads(grad_out, n_head, values.shape[1]).reshape(tok_rows, head_group, HD)
        state_term = jnp.einsum("hds,she->hde", k, v, preferred_element_type=f32)
        adj_term = jnp.einsum("hdt,the->hde", q, g, preferred_element_type=f32)
        state, adjoint = carried_sums(state_term, adj_term, n_ctx)

        keep = token_mask(tile_mask[0], tok_rows // tile_mask.shape[1])
        pair = jnp.einsum("the,she->hts", g, v, preferred_element_type=f32)
        grad_w = (att_scale * pair * keep).astype(bf16)
        spk = jnp.einsum("hdt,hds->hts", q, k, preferred_element_type=f32)
        att_w = (att_scale * spk * keep).astype(bf16)
        query_grad = jnp.einsum("hts,hds->thd", grad_w, k, preferred_element_type=f32) + att_scale * jnp.einsum(
            "the,hde->thd", g, state, preferred_element_type=f32
        )
        key_grad = jnp.einsum("hts,hdt->shd", grad_w, q, preferred_element_type=f32) + att_scale * jnp.einsum(
            "she,hde->shd", v, adjoint, preferred_element_type=f32
        )
        value_grad = jnp.einsum("hts,the->she", att_w, g, preferred_element_type=f32) + att_scale * jnp.einsum(
            "hds,hde->she", k, adjoint, preferred_element_type=f32
        )
        shape = (tok_rows, head_group * HD)
        return (
            query_grad.astype(bf16).reshape(shape),
            key_grad.astype(bf16).reshape(shape),
            value_grad.astype(bf16).reshape(shape),
        )

    return local


def ctx_sizes(devices):
    n_ctx = devices.shape[1]
    n_core = 2
    try:
        n_y = len({d.coords[1] for d in devices[0]})
    except Exception:
        n_y = 8
    if n_y <= 0 or n_ctx % (n_core * n_y) != 0:
        n_y = 8
    return (n_ctx // (n_core * n_y), n_y, n_core)


def solution(mesh):
    devices = np.asarray(mesh.devices)
    sizes = ctx_sizes(devices)
    n_head = devices.shape[0]
    fine = Mesh(devices.reshape((n_head,) + sizes), ("head",) + CTX)
    return jax.shard_map(
        make_local(sizes, n_head),
        mesh=fine,
        in_specs=(
            P("head", CTX),
            P("head", CTX),
            P(CTX, "head"),
            P(CTX, "head", None),
            P(CTX, None, None),
        ),
        out_specs=(P(CTX, "head"), P(CTX, "head"), P(CTX, "head")),
        check_vma=False,
    )
```

profile of v0, /device:TPU:1, one launch (start us, length us, event | category | flops | bytes accessed | tf_op | source)
XLA Modules:
  0.0 78.5 jit_solution(13129867460499165738)
XLA Ops:
  0.6 1.1 %copy.30 = bf16[4,8,8,512]{3,2,1,0:T(8,128)(2,1)S(1)} copy(bf16[4,8,8,512]{3,1,2,0:T(8,128)(2,1)} %bitcast.95) | data formatting | bytes 524288
  1.7 0.8 copy.52
  2.5 11.0 %all-to-all-start = ((bf16[8,32,512]{2,1,0:T(8,128)(2,1)}), bf16[8,32,512]{2,1,0:T(8,128)(2,1)S(1)}, u32[]{:S(2)}, u32[]{:S(2)}) async-start(bf16[8,32,512]{2,1,0:T(8,128)(2,1)} %bitcast.85), calls=%async_computation | async-start | bytes 524288 | tf_op jit(solution)/shard_map/all_to_all | solution.py:36
  13.8 0.2 fusion.19
  14.0 10.0 %all-to-all-done = bf16[8,32,512]{2,1,0:T(8,128)(2,1)S(1)} async-done(((bf16[8,32,512]{2,1,0:T(8,128)(2,1)}), bf16[8,32,512]{2,1,0:T(8,128)(2,1)S(1)}, u32[]{:S(2)}, u32[]{:S(2)}) %all-to-all-start) | async-done | bytes 262176 | tf_op jit(solution)/shard_map/all_to_all | solution.py:36
  24.2 0.2 fusion.30
  24.5 0.8 %pad_maximum_fusion = f32[8,128,128]{2,1,0:T(8,128)} fusion(f32[4,128,128]{2,1,0:T(8,128)S(1)} %fusion.30, f32[4,128,128]{2,1,0:T(8,128)S(1)} %fusion.19), kind=kLoop, calls=%fused_computation.19 | loop fusion | flops 131072 | bytes 1048576 | tf_op jit(solution)/shard_map/concatenate | solution.py:43
  25.3 12.4 %all-to-all-start.1 = ((f32[64,16,128]{2,1,0:T(8,128)}), f32[64,16,128]{2,1,0:T(8,128)S(1)}, u32[]{:S(2)}, u32[]{:S(2)}) async-start(f32[64,16,128]{2,1,0:T(8,128)} %bitcast.6), calls=%async_computation.1 | async-start | bytes 1048576 | tf_op jit(solution)/shard_map/all_to_all | solution.py:44
  37.8 0.7 copy-done.3
  38.6 16.4 %all-to-all-done.1 = f32[64,16,128]{2,1,0:T(8,128)S(1)} async-done(((f32[64,16,128]{2,1,0:T(8,128)}), f32[64,16,128]{2,1,0:T(8,128)S(1)}, u32[]{:S(2)}, u32[]{:S(2)}) %all-to-all-start.1) | async-done | bytes 524320 | tf_op jit(solution)/shard_map/all_to_all | solution.py:44
  55.1 0.6 fusion.9
  55.6 0.7 copy.33
  56.4 6.3 %all-to-all-start.2 = ((bf16[64,16,128]{2,1,0:T(8,128)(2,1)}), bf16[64,16,128]{2,1,0:T(8,128)(2,1)S(1)}, u32[]{:S(2)}, u32[]{:S(2)}) async-start(bf16[64,16,128]{2,1,0:T(8,128)(2,1)} %bitcast.29), calls=%async_computation.2 | async-start | bytes 524288 | tf_op jit(solution)/shard_map/all_to_all | solution.py:52
  62.7 0.3 fusion
  63.0 0.3 fusion.29
  63.3 0.2 fusion.31
  63.6 11.1 %all-to-all-done.2 = bf16[64,16,128]{2,1,0:T(8,128)(2,1)S(1)} async-done(((bf16[64,16,128]{2,1,0:T(8,128)(2,1)}), bf16[64,16,128]{2,1,0:T(8,128)(2,1)S(1)}, u32[]{:S(2)}, u32[]{:S(2)}) %all-to-all-start.2) | async-done | bytes 262176 | tf_op jit(solution)/shard_map/all_to_all | solution.py:52
  74.7 0.3 fusion.3
  74.9 0.5 fusion.8
  75.5 0.8 %copy.27 = bf16[256,512]{1,0:T(8,128)(2,1)} copy(bf16[256,512]{0,1:T(8,128)(2,1)S(1)} %bitcast.89) | data formatting | bytes 524288
  76.3 0.2 fusion.6
  76.5 0.8 %copy.25 = bf16[256,512]{1,0:T(8,128)(2,1)} copy(bf16[256,512]{0,1:T(8,128)(2,1)S(1)} %bitcast.92) | data formatting | bytes 524288
  77.4 0.2 fusion.7
  77.6 0.8 %copy.26 = bf16[256,512]{1,0:T(8,128)(2,1)} copy(bf16[256,512]{0,1:T(8,128)(2,1)S(1)} %bitcast.93) | data formatting | bytes 524288
  (16 shorter events, 0.7 us)
Async XLA Ops:
  0.6 13.2 %copy-start = (bf16[256,512]{1,0:T(8,128)(2,1)S(1)}, bf16[256,512]{1,0:T(8,128)(2,1)}, u32[]{:S(2)}) copy-start(bf16[256,512]{1,0:T(8,128)(2,1)} %param.7) | copy-start | bytes 786436
  2.5 11.1 %copy-start.1 = (s32[32,256]{1,0:T(8,128)S(1)}, s32[32,256]{1,0:T(8,128)}, u32[]{:S(2)}) copy-start(s32[32,256]{1,0:T(8,128)} %param.5) | copy-start | bytes 98308
  2.5 11.1 %copy-start.2 = (s32[32,256]{1,0:T(8,128)S(1)}, s32[32,256]{1,0:T(8,128)}, u32[]{:S(2)}) copy-start(s32[32,256]{1,0:T(8,128)} %param.6) | copy-start | bytes 98308
  2.5 21.5 %all-to-all-start = ((bf16[8,32,512]{2,1,0:T(8,128)(2,1)}), bf16[8,32,512]{2,1,0:T(8,128)(2,1)S(1)}, u32[]{:S(2)}, u32[]{:S(2)}) async-start(bf16[8,32,512]{2,1,0:T(8,128)(2,1)} %bitcast.85), calls=%async_computation | async-start | bytes 524288 | tf_op jit(solution)/shard_map/all_to_all | solution.py:36
  25.3 29.7 %all-to-all-start.1 = ((f32[64,16,128]{2,1,0:T(8,128)}), f32[64,16,128]{2,1,0:T(8,128)S(1)}, u32[]{:S(2)}, u32[]{:S(2)}) async-start(f32[64,16,128]{2,1,0:T(8,128)} %bitcast.6), calls=%async_computation.1 | async-start | bytes 1048576 | tf_op jit(solution)/shard_map/all_to_all | solution.py:44
  37.8 0.7 copy-start.3
  56.4 18.3 %all-to-all-start.2 = ((bf16[64,16,128]{2,1,0:T(8,128)(2,1)}), bf16[64,16,128]{2,1,0:T(8,128)(2,1)S(1)}, u32[]{:S(2)}, u32[]{:S(2)}) async-start(bf16[64,16,128]{2,1,0:T(8,128)(2,1)} %bitcast.29), calls=%async_computation.2 | async-start | bytes 524288 | tf_op jit(solution)/shard_map/all_to_all | solution.py:52
where the time goes:
time: 78.9 us; the launch traced here: 78.5 us
  waiting for transfers between devices  37.5 us (48%)
  starting transfers between devices  29.7 us (38%)
  local copies, waits for them, and re-layouts  6.3 us (8%)
  matrix products  3.1 us (4%)
  other arithmetic  1.06 us (1%)
  between operations  0.8 us (1%)
    all_to_all x1, waiting for transfers between devices, carried_sums(): got = lax.all_to_all(terms, CTX, 0, 0, tiled=True)  16.4 us
    all_to_all x1, starting transfers between devices, carried_sums(): got = lax.all_to_all(terms, CTX, 0, 0, tiled=True)  12.4 us
    all_to_all x1, waiting for transfers between devices, carried_sums(): lax.all_to_all(sums.astype(jnp.bfloat16).reshape(n_ctx, -1, HD), CTX, 0,...  11.1 us
    all_to_all x1, starting transfers between devices, gather_heads(): got = lax.all_to_all(blocks, 'head', 0, 0, tiled=True)  11 us
    all_to_all x1, waiting for transfers between devices, gather_heads(): got = lax.all_to_all(blocks, 'head', 0, 0, tiled=True)  9.98 us
    all_to_all x1, starting transfers between devices, carried_sums(): lax.all_to_all(sums.astype(jnp.bfloat16).reshape(n_ctx, -1, HD), CTX, 0,...  6.29 us
    unnamed x13, local copies, waits for them, and re-layouts  5.04 us
  transfers between devices with their start and end apart: 3, of which 3 were waited for; matrix products, arithmetic and copies ran while one was open for 2% of the time, Pallas kernels for 0%

commit v1 on v0

--- a/solution.py
+++ b/solution.py
@@ -9,6 +9,7 @@
 
 HD = 128
 CTX = ("x", "y", "core")
+CHIPS = ("x", "y")
 
 def unpack_bits(packed, heads_here):
     shifts = jnp.arange(16, dtype=jnp.int32).reshape(1, 1, 16, 1)
@@ -37,21 +38,31 @@
     return got.reshape(n_head * tok_part, width)
 
 
-def carried_sums(state_term, adj_term, n_ctx):
+def swap_core(a):
+    return lax.ppermute(a, "core", [(0, 1), (1, 0)])
+
+
+def carried_sums(state_term, adj_term, n_chip):
     f32 = jnp.float32
     heads = state_term.shape[0]
-    terms = jnp.concatenate([state_term, adj_term], axis=0).reshape(n_ctx, -1, HD)
-    got = lax.all_to_all(terms, CTX, 0, 0, tiled=True)
-    me = lax.axis_index(CTX)
-    row = jnp.arange(n_ctx, dtype=jnp.int32)[:, None]
-    col = jnp.arange(n_ctx, dtype=jnp.int32)[None, :]
-    mix = jnp.where(me < n_ctx // 2, col < row, col > row).astype(f32)
+    core = lax.axis_index("core")
+    other_s = swap_core(state_term)
+    other_a = swap_core(adj_term)
+    chip = jnp.stack([state_term + other_s, adj_term + other_a]).reshape(2, n_chip, -1, HD)
+    mine = lax.dynamic_index_in_dim(chip, core, 0, keepdims=False)
+    got = lax.all_to_all(mine, CHIPS, 0, 0, tiled=True)
+    row = jnp.arange(n_chip, dtype=jnp.int32)[:, None]
+    col = jnp.arange(n_chip, dtype=jnp.int32)[None, :]
+    mix = jnp.where(core == 0, col < row, col > row).astype(f32)
     sums = jnp.dot(
-        mix, got.reshape(n_ctx, -1), precision=lax.Precision.HIGHEST, preferred_element_type=f32
+        mix, got.reshape(n_chip, -1), precision=lax.Precision.HIGHEST, preferred_element_type=f32
     )
-    back = lax.all_to_all(sums.astype(jnp.bfloat16).reshape(n_ctx, -1, HD), CTX, 0, 0, tiled=True)
-    both = back.reshape(2, heads, HD, HD)
-    return both[0], both[1]
+    back = lax.all_to_all(sums.reshape(n_chip, -1, HD), CHIPS, 0, 0, tiled=True)
+    mine_p = back.reshape(heads, HD, HD)
+    other_p = swap_core(mine_p)
+    state_p = jnp.where(core == 0, mine_p, other_p) + jnp.where(core == 1, other_s, 0.0)
+    adj_p = jnp.where(core == 0, other_p, mine_p) + jnp.where(core == 0, other_a, 0.0)
+    return state_p.astype(jnp.bfloat16), adj_p.astype(jnp.bfloat16)
 
 
 def make_local(sizes, n_head):
@@ -69,7 +80,7 @@
         g = gather_heads(grad_out, n_head, values.shape[1]).reshape(tok_rows, head_group, HD)
         state_term = jnp.einsum("hds,she->hde", k, v, preferred_element_type=f32)
         adj_term = jnp.einsum("hdt,the->hde", q, g, preferred_element_type=f32)
-        state, adjoint = carried_sums(state_term, adj_term, n_ctx)
+        state, adjoint = carried_sums(state_term, adj_term, n_ctx // sizes[2])
 
         keep = token_mask(tile_mask[0], tok_rows // tile_mask.shape[1])
         pair = jnp.einsum("the,she->hts", g, v, preferred_element_type=f32)

time: 78.9 us -> 81.9 us (1.038)
  starting transfers between devices: 29.7 us -> 40.1 us
  waiting for transfers between devices: 37.5 us -> 27.6 us
  local copies, waits for them, and re-layouts: 6.3 us -> 8.1 us
    ppermute x0 -> x3, starting transfers between devices: none -> 12.6 us  [swap_core(): return lax.ppermute(a, 'core', [(0, 1), (1, 0)])]
    all_to_all x2, waiting for transfers between devices: 27.5 us -> 18.8 us  [the longest x1 9.67 us: carried_sums(): got = lax.all_to_all(mine, CHIPS, 0, 0, tiled=True)]
    all_to_all x1, waiting for transfers between devices: 9.98 us -> 7.11 us  [gather_heads(): got = lax.all_to_all(blocks, 'head', 0, 0, tiled=True)]
    all_to_all x2, starting transfers between devices: 18.7 us -> 16.5 us  [the longest x1 9.67 us: carried_sums(): got = lax.all_to_all(mine, CHIPS, 0, 0, tiled=True)]
    ppermute x0 -> x3, waiting for transfers between devices: none -> 1.67 us  [swap_core(): return lax.ppermute(a, 'core', [(0, 1), (1, 0)])]
    unnamed x13 -> x20, local copies, waits for them, and re-layouts: 5.04 us -> 6 us
    dot_general x0 -> x1, local copies, waits for them, and re-layouts: none -> 0.86 us  [carried_sums(): jnp.dot(mix, got.reshape(n_chip, -1), precision=lax.Precision.HIGHEST, pr...]
    concatenate x1 -> x0, other arithmetic: 0.83 us -> none  [carried_sums(): jnp.concatenate([state_term, adj_term], axis=0).reshape(n_ctx, -1, HD)]
  transfers between devices with their start and end apart: 3 -> 6, of which waited for: 3 -> 5; matrix products, arithmetic and copies ran while one was open for 2% -> 2% of each run, Pallas kernels for 0% -> 0%
where the time goes in v1:
time: 81.9 us; the launch traced here: 81.3 us
  starting transfers between devices  40.1 us (49%)
  waiting for transfers between devices  27.6 us (34%)
  local copies, waits for them, and re-layouts  8.1 us (10%)
  matrix products  3.6 us (4%)
  other arithmetic  1.08 us (1%)
  between operations  0.85 us (1%)
    ppermute x3, starting transfers between devices, swap_core(): return lax.ppermute(a, 'core', [(0, 1), (1, 0)])  12.6 us
    all_to_all x1, starting transfers between devices, gather_heads(): got = lax.all_to_all(blocks, 'head', 0, 0, tiled=True)  11 us
    all_to_all x1, starting transfers between devices, carried_sums(): got = lax.all_to_all(mine, CHIPS, 0, 0, tiled=True)  9.67 us
    all_to_all x1, waiting for transfers between devices, carried_sums(): got = lax.all_to_all(mine, CHIPS, 0, 0, tiled=True)  9.67 us
    all_to_all x1, waiting for transfers between devices, carried_sums(): back = lax.all_to_all(sums.reshape(n_chip, -1, HD), CHIPS, 0, 0, tiled=True)  9.11 us
    all_to_all x1, waiting for transfers between devices, gather_heads(): got = lax.all_to_all(blocks, 'head', 0, 0, tiled=True)  7.11 us
    all_to_all x1, starting transfers between devices, carried_sums(): back = lax.all_to_all(sums.reshape(n_chip, -1, HD), CHIPS, 0, 0, tiled=True)  6.84 us
    unnamed x20, local copies, waits for them, and re-layouts  6 us
  transfers between devices with their start and end apart: 6, of which 5 were waited for; matrix products, arithmetic and copies ran while one was open for 2% of the time, Pallas kernels for 0%

profile of v1, /device:TPU:1, one launch (start us, length us, event | category | flops | bytes accessed | tf_op | source)
XLA Modules:
  0.0 81.3 jit_solution(6116955267170034532)
XLA Ops:
  0.6 1.1 %copy.50 = bf16[4,8,8,512]{3,2,1,0:T(8,128)(2,1)S(1)} copy(bf16[4,8,8,512]{3,1,2,0:T(8,128)(2,1)} %bitcast.109) | data formatting | bytes 524288
  1.7 0.8 copy.74
  2.5 11.0 %all-to-all-start = ((bf16[8,32,512]{2,1,0:T(8,128)(2,1)}), bf16[8,32,512]{2,1,0:T(8,128)(2,1)S(1)}, u32[]{:S(2)}, u32[]{:S(2)}) async-start(bf16[8,32,512]{2,1,0:T(8,128)(2,1)} %bitcast.96), calls=%async_computation | async-start | bytes 524288 | tf_op jit(solution)/shard_map/all_to_all | solution.py:37
  14.0 2.9 %collective-permute-start = (f32[4,128,128]{2,1,0:T(8,128)S(1)}, f32[4,128,128]{2,1,0:T(8,128)S(1)}, u32[]{:S(2)}, u32[]{:S(2)}) collective-permute-start(f32[4,128,128]{2,1,0:T(8,128)S(1)} %fusion.21), channel_id=1, source_target_pairs={{0,1},{1,0},{2,3},{3,2},{4,5},{5,4},{6,7},{7,6},{8,9},{9,8},{10,11... | collective-permute-start | bytes 786440 | tf_op jit(solution)/shard_map/ppermute | solution.py:42
  16.9 7.1 %all-to-all-done = bf16[8,32,512]{2,1,0:T(8,128)(2,1)S(1)} async-done(((bf16[8,32,512]{2,1,0:T(8,128)(2,1)}), bf16[8,32,512]{2,1,0:T(8,128)(2,1)S(1)}, u32[]{:S(2)}, u32[]{:S(2)}) %all-to-all-start) | async-done | bytes 262176 | tf_op jit(solution)/shard_map/all_to_all | solution.py:37
  24.5 4.2 %collective-permute-start.1 = (f32[4,128,128]{2,1,0:T(8,128)S(1)}, f32[4,128,128]{2,1,0:T(8,128)S(1)}, u32[]{:S(2)}, u32[]{:S(2)}) collective-permute-start(f32[4,128,128]{2,1,0:T(8,128)S(1)} %fusion.36), channel_id=1, source_target_pairs={{0,1},{1,0},{2,3},{3,2},{4,5},{5,4},{6,7},{7,6},{8,9},{9,8},{10,11... | collective-permute-start | bytes 786440 | tf_op jit(solution)/shard_map/ppermute | solution.py:42
  28.8 1.1 %collective-permute-done.1 = f32[4,128,128]{2,1,0:T(8,128)S(1)} collective-permute-done((f32[4,128,128]{2,1,0:T(8,128)S(1)}, f32[4,128,128]{2,1,0:T(8,128)S(1)}, u32[]{:S(2)}, u32[]{:S(2)}) %collective-permute-start.1) | collective-permute-done | bytes 262176 | tf_op jit(solution)/shard_map/ppermute | solution.py:42
  29.9 0.7 copy-done.1
  30.6 0.7 fusion.15
  31.3 9.7 %all-to-all-start.1 = ((f32[32,16,128]{2,1,0:T(8,128)}), f32[32,16,128]{2,1,0:T(8,128)S(1)}, u32[]{:S(2)}, u32[]{:S(2)}) async-start(f32[32,16,128]{2,1,0:T(8,128)} %fusion.15), calls=%async_computation.1 | async-start | bytes 524288 | tf_op jit(solution)/shard_map/all_to_all | solution.py:53
  41.0 9.7 %all-to-all-done.1 = f32[32,16,128]{2,1,0:T(8,128)S(1)} async-done(((f32[32,16,128]{2,1,0:T(8,128)}), f32[32,16,128]{2,1,0:T(8,128)S(1)}, u32[]{:S(2)}, u32[]{:S(2)}) %all-to-all-start.1) | async-done | bytes 262176 | tf_op jit(solution)/shard_map/all_to_all | solution.py:53
  50.7 0.4 fusion.17
  51.0 0.9 %copy.37 = f32[32,16,128]{2,1,0:T(8,128)} copy(f32[32,16,128]{2,0,1:T(8,128)S(1)} %fusion.17) | data formatting | bytes 524288 | tf_op jit(solution)/shard_map/dot_general | solution.py:57
  51.9 6.8 %all-to-all-start.2 = ((f32[32,16,128]{2,1,0:T(8,128)}), f32[32,16,128]{2,1,0:T(8,128)S(1)}, u32[]{:S(2)}, u32[]{:S(2)}) async-start(f32[32,16,128]{2,1,0:T(8,128)} %copy.37), calls=%async_computation.2 | async-start | bytes 524288 | tf_op jit(solution)/shard_map/all_to_all | solution.py:60
  58.9 0.3 fusion
  59.3 9.1 %all-to-all-done.2 = f32[32,16,128]{2,1,0:T(8,128)S(1)} async-done(((f32[32,16,128]{2,1,0:T(8,128)}), f32[32,16,128]{2,1,0:T(8,128)S(1)}, u32[]{:S(2)}, u32[]{:S(2)}) %all-to-all-start.2) | async-done | bytes 262176 | tf_op jit(solution)/shard_map/all_to_all | solution.py:60
  68.4 5.5 %collective-permute-start.2 = (f32[4,128,128]{2,1,0:T(8,128)S(1)}, f32[4,128,128]{2,1,0:T(8,128)S(1)}, u32[]{:S(2)}, u32[]{:S(2)}) collective-permute-start(f32[4,128,128]{2,1,0:T(8,128)S(1)} %bitcast.98), channel_id=1, source_target_pairs={{0,1},{1,0},{2,3},{3,2},{4,5},{5,4},{6,7},{7,6},{8,9},{9,8},{10,11... | collective-permute-start | bytes 786440 | tf_op jit(solution)/shard_map/ppermute | solution.py:42
  74.2 0.3 fusion.35
  74.5 0.6 collective-permute-done.2
  75.2 0.6 copy-done.3
  76.0 1.2 %fusion.8 = bf16[256,4,128]{0,2,1:T(8,128)(2,1)} fusion(f32[256,4,128]{0,2,1:T(8,128)S(1)} %fusion.3, bf16[256,4,128]{0,2,1:T(8,128)(2,1)S(1)} %copy.41, bf16[4,128,256]{2,1,0:T(8,128)(2,1)S(1)} %get-tuple-element.12, bf16[4,128,256]{2,1,0:T(8,128)(2,1)S(1)} %get-tuple-element.13, f32[256,256]{1,0:T(8,128)S(1)} %fusion.16), kind=kOutput, calls=%fused_computation.14 | convolution fusion | flops 135004160 | bytes 1835008 | tf_op jit(solution)/shard_map/hts,the->she/dot_general | solution.py:96
  77.3 1.8 %copy.45 = bf16[256,512]{1,0:T(8,128)(2,1)} copy(bf16[256,512]{0,1:T(8,128)(2,1)} %bitcast.102) | data formatting | bytes 524288
  79.3 0.8 %copy.44 = bf16[256,512]{1,0:T(8,128)(2,1)} copy(bf16[256,512]{0,1:T(8,128)(2,1)S(1)} %bitcast.108) | data formatting | bytes 524288
  80.5 0.8 %copy.43 = bf16[256,512]{1,0:T(8,128)(2,1)} copy(bf16[256,512]{0,1:T(8,128)(2,1)S(1)} %bitcast.101) | data formatting | bytes 524288
  (32 shorter events, 2.4 us)
Async XLA Ops:
  0.6 13.2 %copy-start = (bf16[256,512]{1,0:T(8,128)(2,1)S(1)}, bf16[256,512]{1,0:T(8,128)(2,1)}, u32[]{:S(2)}) copy-start(bf16[256,512]{1,0:T(8,128)(2,1)} %param.7) | copy-start | bytes 786436
  2.5 11.1 %copy-start.5 = (s32[32,256]{1,0:T(8,128)S(1)}, s32[32,256]{1,0:T(8,128)}, u32[]{:S(2)}) copy-start(s32[32,256]{1,0:T(8,128)} %param.5) | copy-start | bytes 98308
  2.5 11.1 %copy-start.6 = (s32[32,256]{1,0:T(8,128)S(1)}, s32[32,256]{1,0:T(8,128)}, u32[]{:S(2)}) copy-start(s32[32,256]{1,0:T(8,128)} %param.6) | copy-start | bytes 98308
  2.5 21.5 %all-to-all-start = ((bf16[8,32,512]{2,1,0:T(8,128)(2,1)}), bf16[8,32,512]{2,1,0:T(8,128)(2,1)S(1)}, u32[]{:S(2)}, u32[]{:S(2)}) async-start(bf16[8,32,512]{2,1,0:T(8,128)(2,1)} %bitcast.96), calls=%async_computation | async-start | bytes 524288 | tf_op jit(solution)/shard_map/all_to_all | solution.py:37
  14.0 14.7 %collective-permute-start = (f32[4,128,128]{2,1,0:T(8,128)S(1)}, f32[4,128,128]{2,1,0:T(8,128)S(1)}, u32[]{:S(2)}, u32[]{:S(2)}) collective-permute-start(f32[4,128,128]{2,1,0:T(8,128)S(1)} %fusion.21), channel_id=1, source_target_pairs={{0,1},{1,0},{2,3},{3,2},{4,5},{5,4},{6,7},{7,6},{8,9},{9,8},{10,11... | collective-permute-start | bytes 786440 | tf_op jit(solution)/shard_map/ppermute | solution.py:42
  24.5 5.4 %collective-permute-start.1 = (f32[4,128,128]{2,1,0:T(8,128)S(1)}, f32[4,128,128]{2,1,0:T(8,128)S(1)}, u32[]{:S(2)}, u32[]{:S(2)}) collective-permute-start(f32[4,128,128]{2,1,0:T(8,128)S(1)} %fusion.36), channel_id=1, source_target_pairs={{0,1},{1,0},{2,3},{3,2},{4,5},{5,4},{6,7},{7,6},{8,9},{9,8},{10,11... | collective-permute-start | bytes 786440 | tf_op jit(solution)/shard_map/ppermute | solution.py:42
  29.9 0.7 copy-start.1
  31.3 19.4 %all-to-all-start.1 = ((f32[32,16,128]{2,1,0:T(8,128)}), f32[32,16,128]{2,1,0:T(8,128)S(1)}, u32[]{:S(2)}, u32[]{:S(2)}) async-start(f32[32,16,128]{2,1,0:T(8,128)} %fusion.15), calls=%async_computation.1 | async-start | bytes 524288 | tf_op jit(solution)/shard_map/all_to_all | solution.py:53
  51.9 6.9 %copy-start.7 = (s32[1,2,2]{2,1,0:T(2,128)S(1)}, s32[1,2,2]{2,1,0:T(2,128)}, u32[]{:S(2)}) copy-start(s32[1,2,2]{2,1,0:T(2,128)} %param.9) | copy-start | bytes 52
  51.9 16.5 %all-to-all-start.2 = ((f32[32,16,128]{2,1,0:T(8,128)}), f32[32,16,128]{2,1,0:T(8,128)S(1)}, u32[]{:S(2)}, u32[]{:S(2)}) async-start(f32[32,16,128]{2,1,0:T(8,128)} %copy.37), calls=%async_computation.2 | async-start | bytes 524288 | tf_op jit(solution)/shard_map/all_to_all | solution.py:60
  68.4 6.7 %collective-permute-start.2 = (f32[4,128,128]{2,1,0:T(8,128)S(1)}, f32[4,128,128]{2,1,0:T(8,128)S(1)}, u32[]{:S(2)}, u32[]{:S(2)}) collective-permute-start(f32[4,128,128]{2,1,0:T(8,128)S(1)} %bitcast.98), channel_id=1, source_target_pairs={{0,1},{1,0},{2,3},{3,2},{4,5},{5,4},{6,7},{7,6},{8,9},{9,8},{10,11... | collective-permute-start | bytes 786440 | tf_op jit(solution)/shard_map/ppermute | solution.py:42
  74.2 1.0 %copy-start.2 = (f32[4,128,128]{2,1,0:T(8,128)S(1)}, f32[4,128,128]{2,1,0:T(8,128)}, u32[]{:S(2)}) copy-start(f32[4,128,128]{2,1,0:T(8,128)} %copy-done.1) | copy-start | bytes 786436
  75.1 0.7 copy-start.3
  79.3 1.0 %copy-start.4 = (f32[4,128,128]{2,1,0:T(8,128)S(1)}, f32[4,128,128]{2,1,0:T(8,128)}, u32[]{:S(2)}) copy-start(f32[4,128,128]{2,1,0:T(8,128)} %copy-done.3) | copy-start | bytes 786436

commit v2 on v1

--- a/solution.py
+++ b/solution.py
@@ -42,22 +42,29 @@
     return lax.ppermute(a, "core", [(0, 1), (1, 0)])
 
 
-def carried_sums(state_term, adj_term, n_chip):
+def carried_sums(state_term, adj_term, sizes):
     f32 = jnp.float32
+    n_x, n_y, _ = sizes
     heads = state_term.shape[0]
     core = lax.axis_index("core")
+    me_x = lax.axis_index("x")
     other_s = swap_core(state_term)
     other_a = swap_core(adj_term)
-    chip = jnp.stack([state_term + other_s, adj_term + other_a]).reshape(2, n_chip, -1, HD)
+    chip = jnp.stack([state_term + other_s, adj_term + other_a]).reshape(2, n_y, -1, HD)
     mine = lax.dynamic_index_in_dim(chip, core, 0, keepdims=False)
-    got = lax.all_to_all(mine, CHIPS, 0, 0, tiled=True)
-    row = jnp.arange(n_chip, dtype=jnp.int32)[:, None]
-    col = jnp.arange(n_chip, dtype=jnp.int32)[None, :]
+    got = lax.all_to_all(mine, "y", 0, 0, tiled=True)
+    row = jnp.arange(n_y, dtype=jnp.int32)[:, None]
+    col = jnp.arange(n_y, dtype=jnp.int32)[None, :]
     mix = jnp.where(core == 0, col < row, col > row).astype(f32)
-    sums = jnp.dot(
-        mix, got.reshape(n_chip, -1), precision=lax.Precision.HIGHEST, preferred_element_type=f32
-    )
-    back = lax.all_to_all(sums.reshape(n_chip, -1, HD), CHIPS, 0, 0, tiled=True)
+    flat = got.reshape(n_y, -1)
+    in_row = jnp.dot(mix, flat, precision=lax.Precision.HIGHEST, preferred_element_type=f32)
+    total = jnp.sum(got, axis=0)
+    totals = lax.all_to_all(jnp.broadcast_to(total, (n_x,) + total.shape), "x", 0, 0, tiled=True)
+    x_index = jnp.arange(n_x, dtype=jnp.int32)
+    x_keep = jnp.where(core == 0, x_index < me_x, x_index > me_x)
+    over_rows = jnp.sum(jnp.where(x_keep[:, None, None], totals, 0.0), axis=0)
+    sums = in_row.reshape(got.shape) + over_rows[None]
+    back = lax.all_to_all(sums, "y", 0, 0, tiled=True)
     mine_p = back.reshape(heads, HD, HD)
     other_p = swap_core(mine_p)
     state_p = jnp.where(core == 0, mine_p, other_p) + jnp.where(core == 1, other_s, 0.0)
@@ -80,7 +87,7 @@
         g = gather_heads(grad_out, n_head, values.shape[1]).reshape(tok_rows, head_group, HD)
         state_term = jnp.einsum("hds,she->hde", k, v, preferred_element_type=f32)
         adj_term = jnp.einsum("hdt,the->hde", q, g, preferred_element_type=f32)
-        state, adjoint = carried_sums(state_term, adj_term, n_ctx // sizes[2])
+        state, adjoint = carried_sums(state_term, adj_term, sizes)
 
         keep = token_mask(tile_mask[0], tok_rows // tile_mask.shape[1])
         pair = jnp.einsum("the,she->hts", g, v, preferred_element_type=f32)

time: 81.9 us -> 87 us (1.062)
  waiting for transfers between devices: 27.6 us -> 32.9 us
  starting transfers between devices: 40.1 us -> 38.4 us
  local copies, waits for them, and re-layouts: 8.1 us -> 9.33 us
    all_to_all x2 -> x3, waiting for transfers between devices: 18.8 us -> 24.1 us  [the longest x1 10.4 us: carried_sums(): got = lax.all_to_all(mine, 'y', 0, 0, tiled=True)]
    all_to_all x2 -> x3, starting transfers between devices: 16.5 us -> 14.2 us  [the longest x1 6.82 us: carried_sums(): got = lax.all_to_all(mine, 'y', 0, 0, tiled=True)]
  transfers between devices with their start and end apart: 6 -> 7, of which waited for: 5 -> 6; matrix products, arithmetic and copies ran while one was open for 2% -> 2% of each run, Pallas kernels for 0% -> 0%
where the time goes in v2:
time: 87 us; the launch traced here: 86.3 us
  starting transfers between devices  38.4 us (44%)
  waiting for transfers between devices  32.9 us (38%)
  local copies, waits for them, and re-layouts  9.33 us (11%)
  matrix products  3.64 us (4%)
  other arithmetic  1.18 us (1%)
    ppermute x3, starting transfers between devices, swap_core(): return lax.ppermute(a, 'core', [(0, 1), (1, 0)])  13.2 us
    all_to_all x1, starting transfers between devices, gather_heads(): got = lax.all_to_all(blocks, 'head', 0, 0, tiled=True)  11 us
    all_to_all x1, waiting for transfers between devices, carried_sums(): got = lax.all_to_all(mine, 'y', 0, 0, tiled=True)  10.4 us
    all_to_all x1, waiting for transfers between devices, carried_sums(): back = lax.all_to_all(sums, 'y', 0, 0, tiled=True)  8.83 us
    all_to_all x1, waiting for transfers between devices, gather_heads(): got = lax.all_to_all(blocks, 'head', 0, 0, tiled=True)  7.11 us
    all_to_all x1, starting transfers between devices, carried_sums(): got = lax.all_to_all(mine, 'y', 0, 0, tiled=True)  6.82 us
    unnamed x20, local copies, waits for them, and re-layouts  6.67 us
    all_to_all x1, waiting for transfers between devices, carried_sums(): lax.all_to_all(jnp.broadcast_to(total, (n_x,) + total.shape), 'x', 0, 0,...  4.82 us
  transfers between devices with their start and end apart: 7, of which 6 were waited for; matrix products, arithmetic and copies ran while one was open for 2% of the time, Pallas kernels for 0%

profile of v2, /device:TPU:1, one launch (start us, length us, event | category | flops | bytes accessed | tf_op | source)
XLA Modules:
  0.0 86.3 jit_solution(16027056597145205010)
XLA Ops:
  0.6 1.1 %copy.61 = bf16[4,8,8,512]{3,2,1,0:T(8,128)(2,1)S(1)} copy(bf16[4,8,8,512]{3,1,2,0:T(8,128)(2,1)} %bitcast.105) | data formatting | bytes 524288
  1.7 0.8 copy.82
  2.5 11.0 %all-to-all-start = ((bf16[8,32,512]{2,1,0:T(8,128)(2,1)}), bf16[8,32,512]{2,1,0:T(8,128)(2,1)S(1)}, u32[]{:S(2)}, u32[]{:S(2)}) async-start(bf16[8,32,512]{2,1,0:T(8,128)(2,1)} %bitcast.92), calls=%async_computation | async-start | bytes 524288 | tf_op jit(solution)/shard_map/all_to_all | solution.py:37
  14.0 2.9 %collective-permute-start = (f32[4,128,128]{2,1,0:T(8,128)S(1)}, f32[4,128,128]{2,1,0:T(8,128)S(1)}, u32[]{:S(2)}, u32[]{:S(2)}) collective-permute-start(f32[4,128,128]{2,1,0:T(8,128)S(1)} %fusion.19), channel_id=1, source_target_pairs={{0,1},{1,0},{2,3},{3,2},{4,5},{5,4},{6,7},{7,6},{8,9},{9,8},{10,11... | collective-permute-start | bytes 786440 | tf_op jit(solution)/shard_map/ppermute | solution.py:42
  16.9 7.1 %all-to-all-done = bf16[8,32,512]{2,1,0:T(8,128)(2,1)S(1)} async-done(((bf16[8,32,512]{2,1,0:T(8,128)(2,1)}), bf16[8,32,512]{2,1,0:T(8,128)(2,1)S(1)}, u32[]{:S(2)}, u32[]{:S(2)}) %all-to-all-start) | async-done | bytes 262176 | tf_op jit(solution)/shard_map/all_to_all | solution.py:37
  24.5 4.2 %collective-permute-start.1 = (f32[4,128,128]{2,1,0:T(8,128)S(1)}, f32[4,128,128]{2,1,0:T(8,128)S(1)}, u32[]{:S(2)}, u32[]{:S(2)}) collective-permute-start(f32[4,128,128]{2,1,0:T(8,128)S(1)} %fusion.34), channel_id=1, source_target_pairs={{0,1},{1,0},{2,3},{3,2},{4,5},{5,4},{6,7},{7,6},{8,9},{9,8},{10,11... | collective-permute-start | bytes 786440 | tf_op jit(solution)/shard_map/ppermute | solution.py:42
  28.8 1.1 %collective-permute-done.1 = f32[4,128,128]{2,1,0:T(8,128)S(1)} collective-permute-done((f32[4,128,128]{2,1,0:T(8,128)S(1)}, f32[4,128,128]{2,1,0:T(8,128)S(1)}, u32[]{:S(2)}, u32[]{:S(2)}) %collective-permute-start.1) | collective-permute-done | bytes 262176 | tf_op jit(solution)/shard_map/ppermute | solution.py:42
  29.9 0.7 copy-done.1
  30.6 0.7 fusion.15
  31.3 6.8 %all-to-all-start.1 = ((f32[8,64,128]{2,1,0:T(8,128)}), f32[8,64,128]{2,1,0:T(8,128)S(1)}, u32[]{:S(2)}, u32[]{:S(2)}) async-start(f32[8,64,128]{2,1,0:T(8,128)} %fusion.15), calls=%async_computation.1 | async-start | bytes 524288 | tf_op jit(solution)/shard_map/all_to_all | solution.py:55
  38.1 0.7 copy-done.7
  38.8 10.4 %all-to-all-done.1 = f32[8,64,128]{2,1,0:T(8,128)S(1)} async-done(((f32[8,64,128]{2,1,0:T(8,128)}), f32[8,64,128]{2,1,0:T(8,128)S(1)}, u32[]{:S(2)}, u32[]{:S(2)}) %all-to-all-start.1) | async-done | bytes 262176 | tf_op jit(solution)/shard_map/all_to_all | solution.py:55
  49.3 0.7 broadcast_in_dim.55
  49.9 4.0 %all-to-all-start.2 = ((f32[4,64,128]{2,1,0:T(8,128)}), f32[4,64,128]{2,1,0:T(8,128)S(1)}, u32[]{:S(2)}, u32[]{:S(2)}) async-start(f32[4,64,128]{2,1,0:T(8,128)} %broadcast_in_dim.55), calls=%async_computation.2 | async-start | bytes 262144 | tf_op jit(solution)/shard_map/all_to_all | solution.py:62
  53.9 4.8 %all-to-all-done.2 = f32[4,64,128]{2,1,0:T(8,128)S(1)} async-done(((f32[4,64,128]{2,1,0:T(8,128)}), f32[4,64,128]{2,1,0:T(8,128)S(1)}, u32[]{:S(2)}, u32[]{:S(2)}) %all-to-all-start.2) | async-done | bytes 131104 | tf_op jit(solution)/shard_map/all_to_all | solution.py:62
  59.2 0.8 copy.49
  60.0 3.4 %all-to-all-start.3 = ((f32[8,64,128]{2,1,0:T(8,128)}), f32[8,64,128]{2,1,0:T(8,128)S(1)}, u32[]{:S(2)}, u32[]{:S(2)}) async-start(f32[8,64,128]{2,1,0:T(8,128)} %copy.49), calls=%async_computation.3 | async-start | bytes 524288 | tf_op jit(solution)/shard_map/all_to_all | solution.py:67
  63.9 8.8 %all-to-all-done.3 = f32[8,64,128]{2,1,0:T(8,128)S(1)} async-done(((f32[8,64,128]{2,1,0:T(8,128)}), f32[8,64,128]{2,1,0:T(8,128)S(1)}, u32[]{:S(2)}, u32[]{:S(2)}) %all-to-all-start.3) | async-done | bytes 262176 | tf_op jit(solution)/shard_map/all_to_all | solution.py:67
  72.8 6.1 %collective-permute-start.2 = (f32[4,128,128]{2,1,0:T(8,128)S(1)}, f32[4,128,128]{2,1,0:T(8,128)S(1)}, u32[]{:S(2)}, u32[]{:S(2)}) collective-permute-start(f32[4,128,128]{2,1,0:T(8,128)S(1)} %bitcast.94), channel_id=1, source_target_pairs={{0,1},{1,0},{2,3},{3,2},{4,5},{5,4},{6,7},{7,6},{8,9},{9,8},{10,11... | collective-permute-start | bytes 786440 | tf_op jit(solution)/shard_map/ppermute | solution.py:42
  80.1 0.6 copy-done.3
  81.0 1.2 %fusion.8 = bf16[256,4,128]{0,2,1:T(8,128)(2,1)} fusion(f32[256,4,128]{0,2,1:T(8,128)S(1)} %fusion.3, bf16[256,4,128]{0,2,1:T(8,128)(2,1)S(1)} %copy.53, bf16[4,128,256]{2,1,0:T(8,128)(2,1)S(1)} %get-tuple-element.15, bf16[4,128,256]{2,1,0:T(8,128)(2,1)S(1)} %get-tuple-element.16, f32[256,256]{1,0:T(8,128)S(1)} %fusion.17), kind=kOutput, calls=%fused_computation.14 | convolution fusion | flops 135004160 | bytes 1835008 | tf_op jit(solution)/shard_map/hts,the->she/dot_general | solution.py:103
  82.2 1.8 %copy.57 = bf16[256,512]{1,0:T(8,128)(2,1)} copy(bf16[256,512]{0,1:T(8,128)(2,1)} %bitcast.99) | data formatting | bytes 524288
  84.3 0.8 copy.56
  85.4 0.8 copy.55
  (38 shorter events, 4.1 us)
Async XLA Ops:
  0.6 13.2 %copy-start = (bf16[256,512]{1,0:T(8,128)(2,1)S(1)}, bf16[256,512]{1,0:T(8,128)(2,1)}, u32[]{:S(2)}) copy-start(bf16[256,512]{1,0:T(8,128)(2,1)} %param.7) | copy-start | bytes 786436
  2.5 11.1 %copy-start.5 = (s32[32,256]{1,0:T(8,128)S(1)}, s32[32,256]{1,0:T(8,128)}, u32[]{:S(2)}) copy-start(s32[32,256]{1,0:T(8,128)} %param.5) | copy-start | bytes 98308
  2.5 11.1 %copy-start.6 = (s32[32,256]{1,0:T(8,128)S(1)}, s32[32,256]{1,0:T(8,128)}, u32[]{:S(2)}) copy-start(s32[32,256]{1,0:T(8,128)} %param.6) | copy-start | bytes 98308
  2.5 21.5 %all-to-all-start = ((bf16[8,32,512]{2,1,0:T(8,128)(2,1)}), bf16[8,32,512]{2,1,0:T(8,128)(2,1)S(1)}, u32[]{:S(2)}, u32[]{:S(2)}) async-start(bf16[8,32,512]{2,1,0:T(8,128)(2,1)} %bitcast.92), calls=%async_computation | async-start | bytes 524288 | tf_op jit(solution)/shard_map/all_to_all | solution.py:37
  14.0 14.7 %collective-permute-start = (f32[4,128,128]{2,1,0:T(8,128)S(1)}, f32[4,128,128]{2,1,0:T(8,128)S(1)}, u32[]{:S(2)}, u32[]{:S(2)}) collective-permute-start(f32[4,128,128]{2,1,0:T(8,128)S(1)} %fusion.19), channel_id=1, source_target_pairs={{0,1},{1,0},{2,3},{3,2},{4,5},{5,4},{6,7},{7,6},{8,9},{9,8},{10,11... | collective-permute-start | bytes 786440 | tf_op jit(solution)/shard_map/ppermute | solution.py:42
  24.5 5.4 %collective-permute-start.1 = (f32[4,128,128]{2,1,0:T(8,128)S(1)}, f32[4,128,128]{2,1,0:T(8,128)S(1)}, u32[]{:S(2)}, u32[]{:S(2)}) collective-permute-start(f32[4,128,128]{2,1,0:T(8,128)S(1)} %fusion.34), channel_id=1, source_target_pairs={{0,1},{1,0},{2,3},{3,2},{4,5},{5,4},{6,7},{7,6},{8,9},{9,8},{10,11... | collective-permute-start | bytes 786440 | tf_op jit(solution)/shard_map/ppermute | solution.py:42
  29.9 0.7 copy-start.1
  31.3 17.9 %all-to-all-start.1 = ((f32[8,64,128]{2,1,0:T(8,128)}), f32[8,64,128]{2,1,0:T(8,128)S(1)}, u32[]{:S(2)}, u32[]{:S(2)}) async-start(f32[8,64,128]{2,1,0:T(8,128)} %fusion.15), calls=%async_computation.1 | async-start | bytes 524288 | tf_op jit(solution)/shard_map/all_to_all | solution.py:55
  38.1 0.7 copy-start.7
  49.9 8.8 %all-to-all-start.2 = ((f32[4,64,128]{2,1,0:T(8,128)}), f32[4,64,128]{2,1,0:T(8,128)S(1)}, u32[]{:S(2)}, u32[]{:S(2)}) async-start(f32[4,64,128]{2,1,0:T(8,128)} %broadcast_in_dim.55), calls=%async_computation.2 | async-start | bytes 262144 | tf_op jit(solution)/shard_map/all_to_all | solution.py:62
  60.0 12.8 %all-to-all-start.3 = ((f32[8,64,128]{2,1,0:T(8,128)}), f32[8,64,128]{2,1,0:T(8,128)S(1)}, u32[]{:S(2)}, u32[]{:S(2)}) async-start(f32[8,64,128]{2,1,0:T(8,128)} %copy.49), calls=%async_computation.3 | async-start | bytes 524288 | tf_op jit(solution)/shard_map/all_to_all | solution.py:67
  72.8 7.2 %collective-permute-start.2 = (f32[4,128,128]{2,1,0:T(8,128)S(1)}, f32[4,128,128]{2,1,0:T(8,128)S(1)}, u32[]{:S(2)}, u32[]{:S(2)}) collective-permute-start(f32[4,128,128]{2,1,0:T(8,128)S(1)} %bitcast.94), channel_id=1, source_target_pairs={{0,1},{1,0},{2,3},{3,2},{4,5},{5,4},{6,7},{7,6},{8,9},{9,8},{10,11... | collective-permute-start | bytes 786440 | tf_op jit(solution)/shard_map/ppermute | solution.py:42
  79.1 1.0 %copy-start.2 = (f32[4,128,128]{2,1,0:T(8,128)S(1)}, f32[4,128,128]{2,1,0:T(8,128)}, u32[]{:S(2)}) copy-start(f32[4,128,128]{2,1,0:T(8,128)} %copy-done.1) | copy-start | bytes 786436
  80.0 0.7 copy-start.3
  84.3 1.0 %copy-start.4 = (f32[4,128,128]{2,1,0:T(8,128)S(1)}, f32[4,128,128]{2,1,0:T(8,128)}, u32[]{:S(2)}) copy-start(f32[4,128,128]{2,1,0:T(8,128)} %copy-done.3) | copy-start | bytes 786436

commit v3 on v0

--- a/solution.py
+++ b/solution.py
@@ -66,31 +66,33 @@
         q = unpack_bits(query_bits, head_group)
         k = unpack_bits(key_bits, head_group)
         v = values.reshape(tok_rows, head_group, HD)
-        g = gather_heads(grad_out, n_head, values.shape[1]).reshape(tok_rows, head_group, HD)
+        g2 = gather_heads(grad_out, n_head, values.shape[1])
+        g = g2.reshape(tok_rows, head_group, HD)
         state_term = jnp.einsum("hds,she->hde", k, v, preferred_element_type=f32)
         adj_term = jnp.einsum("hdt,the->hde", q, g, preferred_element_type=f32)
         state, adjoint = carried_sums(state_term, adj_term, n_ctx)
 
         keep = token_mask(tile_mask[0], tok_rows // tile_mask.shape[1])
-        pair = jnp.einsum("the,she->hts", g, v, preferred_element_type=f32)
-        grad_w = (att_scale * pair * keep).astype(bf16)
-        spk = jnp.einsum("hdt,hds->hts", q, k, preferred_element_type=f32)
-        att_w = (att_scale * spk * keep).astype(bf16)
-        query_grad = jnp.einsum("hts,hds->thd", grad_w, k, preferred_element_type=f32) + att_scale * jnp.einsum(
-            "the,hde->thd", g, state, preferred_element_type=f32
-        )
-        key_grad = jnp.einsum("hts,hdt->shd", grad_w, q, preferred_element_type=f32) + att_scale * jnp.einsum(
-            "she,hde->shd", v, adjoint, preferred_element_type=f32
-        )
-        value_grad = jnp.einsum("hts,the->she", att_w, g, preferred_element_type=f32) + att_scale * jnp.einsum(
-            "hds,hde->she", k, adjoint, preferred_element_type=f32
-        )
-        shape = (tok_rows, head_group * HD)
-        return (
-            query_grad.astype(bf16).reshape(shape),
-            key_grad.astype(bf16).reshape(shape),
-            value_grad.astype(bf16).reshape(shape),
-        )
+        outs = ([], [], [])
+        for h in range(head_group):
+            cols = slice(h * HD, (h + 1) * HD)
+            gh = g2[:, cols]
+            vh = values[:, cols]
+            qh = q[h]
+            kh = k[h]
+            pair = lax.dot_general(gh, vh, (((1,), (1,)), ((), ())), preferred_element_type=f32)
+            grad_w = (att_scale * pair * keep).astype(bf16)
+            spk = lax.dot_general(qh, kh, (((0,), (0,)), ((), ())), preferred_element_type=f32)
+            att_w = (att_scale * spk * keep).astype(bf16)
+            qg = lax.dot_general(grad_w, kh, (((1,), (1,)), ((), ())), preferred_element_type=f32)
+            qg = qg + att_scale * lax.dot_general(gh, state[h], (((1,), (1,)), ((), ())), preferred_element_type=f32)
+            kg = lax.dot_general(grad_w, qh, (((0,), (1,)), ((), ())), preferred_element_type=f32)
+            kg = kg + att_scale * lax.dot_general(vh, adjoint[h], (((1,), (1,)), ((), ())), preferred_element_type=f32)
+            vg = lax.dot_general(att_w, gh, (((0,), (0,)), ((), ())), preferred_element_type=f32)
+            vg = vg + att_scale * lax.dot_general(kh, adjoint[h], (((0,), (0,)), ((), ())), preferred_element_type=f32)
+            for out, part in zip(outs, (qg, kg, vg)):
+                out.append(part.astype(bf16))
+        return tuple(jnp.concatenate(out, axis=1) for out in outs)
 
     return local
 

time: 78.9 us -> 82.9 us (1.051)
  matrix products: 3.1 us -> 6.89 us
    dot_general x7 -> x28, matrix products: 2.11 us -> 5.92 us  [the longest x4 1.53 us: local(): lax.dot_general(att_w, gh, (((0,), (0,)), ((), ())), preferred_element_ty...]
    another operation x3 -> x1, local copies, waits for them, and re-layouts: 1.02 us -> 0.06 us  [local(): g = g2.reshape(tok_rows, head_group, HD)]
where the time goes in v3:
time: 82.9 us; the launch traced here: 82.4 us
  waiting for transfers between devices  37.3 us (45%)
  starting transfers between devices  29.9 us (36%)
  matrix products  6.89 us (8%)
  local copies, waits for them, and re-layouts  6.2 us (7%)
  other arithmetic  1.25 us (2%)
  between operations  0.93 us (1%)
    all_to_all x1, waiting for transfers between devices, carried_sums(): got = lax.all_to_all(terms, CTX, 0, 0, tiled=True)  16.7 us
    all_to_all x1, starting transfers between devices, carried_sums(): got = lax.all_to_all(terms, CTX, 0, 0, tiled=True)  12.6 us
    all_to_all x1, waiting for transfers between devices, carried_sums(): lax.all_to_all(sums.astype(jnp.bfloat16).reshape(n_ctx, -1, HD), CTX, 0,...  11.4 us
    all_to_all x1, starting transfers between devices, gather_heads(): got = lax.all_to_all(blocks, 'head', 0, 0, tiled=True)  11 us
    all_to_all x1, waiting for transfers between devices, gather_heads(): got = lax.all_to_all(blocks, 'head', 0, 0, tiled=True)  9.24 us
    all_to_all x1, starting transfers between devices, carried_sums(): lax.all_to_all(sums.astype(jnp.bfloat16).reshape(n_ctx, -1, HD), CTX, 0,...  6.29 us
    unnamed x13, local copies, waits for them, and re-layouts  5.07 us
  transfers between devices with their start and end apart: 3, of which 3 were waited for; matrix products, arithmetic and copies ran while one was open for 2% of the time, Pallas kernels for 0%

profile of v3, /device:TPU:1, one launch (start us, length us, event | category | flops | bytes accessed | tf_op | source)
XLA Modules:
  0.0 82.4 jit_solution(15386856449179630987)
XLA Ops:
  0.6 1.0 %copy.31 = bf16[4,8,8,512]{3,2,1,0:T(8,128)(2,1)S(1)} copy(bf16[4,8,8,512]{3,1,2,0:T(8,128)(2,1)} %bitcast.245) | data formatting | bytes 524288
  1.7 0.8 copy.24
  2.5 11.0 %all-to-all-start = ((bf16[8,32,512]{2,1,0:T(8,128)(2,1)}), bf16[8,32,512]{2,1,0:T(8,128)(2,1)S(1)}, u32[]{:S(2)}, u32[]{:S(2)}) async-start(bf16[8,32,512]{2,1,0:T(8,128)(2,1)} %copy.24), calls=%async_computation | async-start | bytes 524288 | tf_op jit(solution)/shard_map/all_to_all | solution.py:36
  13.7 0.7 copy-done
  14.7 9.2 %all-to-all-done = bf16[8,32,512]{2,1,0:T(8,128)(2,1)S(1)} async-done(((bf16[8,32,512]{2,1,0:T(8,128)(2,1)}), bf16[8,32,512]{2,1,0:T(8,128)(2,1)S(1)}, u32[]{:S(2)}, u32[]{:S(2)}) %all-to-all-start) | async-done | bytes 262176 | tf_op jit(solution)/shard_map/all_to_all | solution.py:36
  24.0 0.2 fusion.58
  24.2 0.8 %pad_maximum_fusion = f32[8,128,128]{2,1,0:T(8,128)} fusion(f32[4,128,128]{2,1,0:T(8,128)S(1)} %fusion.58, f32[4,128,128]{2,1,0:T(8,128)S(1)} %fusion.55), kind=kLoop, calls=%fused_computation.80 | loop fusion | flops 131072 | bytes 1048576 | tf_op jit(solution)/shard_map/concatenate | solution.py:43
  25.1 12.6 %all-to-all-start.1 = ((f32[64,16,128]{2,1,0:T(8,128)}), f32[64,16,128]{2,1,0:T(8,128)S(1)}, u32[]{:S(2)}, u32[]{:S(2)}) async-start(f32[64,16,128]{2,1,0:T(8,128)} %bitcast.8), calls=%async_computation.1 | async-start | bytes 1048576 | tf_op jit(solution)/shard_map/all_to_all | solution.py:44
  38.2 16.7 %all-to-all-done.1 = f32[64,16,128]{2,1,0:T(8,128)S(1)} async-done(((f32[64,16,128]{2,1,0:T(8,128)}), f32[64,16,128]{2,1,0:T(8,128)S(1)}, u32[]{:S(2)}, u32[]{:S(2)}) %all-to-all-start.1) | async-done | bytes 524320 | tf_op jit(solution)/shard_map/all_to_all | solution.py:44
  54.9 0.6 fusion
  55.5 0.7 copy.34
  56.3 6.3 %all-to-all-start.2 = ((bf16[64,16,128]{2,1,0:T(8,128)(2,1)}), bf16[64,16,128]{2,1,0:T(8,128)(2,1)S(1)}, u32[]{:S(2)}, u32[]{:S(2)}) async-start(bf16[64,16,128]{2,1,0:T(8,128)(2,1)} %bitcast.55), calls=%async_computation.2 | async-start | bytes 524288 | tf_op jit(solution)/shard_map/all_to_all | solution.py:52
  63.1 11.4 %all-to-all-done.2 = bf16[64,16,128]{2,1,0:T(8,128)(2,1)S(1)} async-done(((bf16[64,16,128]{2,1,0:T(8,128)(2,1)}), bf16[64,16,128]{2,1,0:T(8,128)(2,1)S(1)}, u32[]{:S(2)}, u32[]{:S(2)}) %all-to-all-start.2) | async-done | bytes 262176 | tf_op jit(solution)/shard_map/all_to_all | solution.py:52
  74.7 0.2 convolution_multiply_fusion.7
  74.9 0.4 fusion.37
  75.5 0.2 convolution_multiply_fusion.6
  75.7 0.4 fusion.38
  76.3 0.2 convolution_multiply_fusion.5
  76.5 0.4 fusion.39
  77.1 0.2 convolution_multiply_fusion.4
  77.3 0.4 fusion.40
  77.7 0.8 %copy.29 = bf16[256,512]{1,0:T(8,128)(2,1)} copy(bf16[256,512]{0,1:T(8,128)(2,1)S(1)} %pad_maximum_fusion.3) | data formatting | bytes 524288
  79.2 0.8 %copy.28 = bf16[256,512]{1,0:T(8,128)(2,1)} copy(bf16[256,512]{0,1:T(8,128)(2,1)S(1)} %pad_maximum_fusion.2) | data formatting | bytes 524288
  81.6 0.8 %copy.27 = bf16[256,512]{1,0:T(8,128)(2,1)} copy(bf16[256,512]{0,1:T(8,128)(2,1)S(1)} %pad_maximum_fusion.1) | data formatting | bytes 524288
  (41 shorter events, 4.5 us)
Async XLA Ops:
  2.4 11.1 %copy-start.1 = (s32[32,256]{1,0:T(8,128)S(1)}, s32[32,256]{1,0:T(8,128)}, u32[]{:S(2)}) copy-start(s32[32,256]{1,0:T(8,128)} %param.6) | copy-start | bytes 98308
  2.5 11.1 %copy-start.2 = (s32[32,256]{1,0:T(8,128)S(1)}, s32[32,256]{1,0:T(8,128)}, u32[]{:S(2)}) copy-start(s32[32,256]{1,0:T(8,128)} %param.5) | copy-start | bytes 98308
  2.5 21.5 %all-to-all-start = ((bf16[8,32,512]{2,1,0:T(8,128)(2,1)}), bf16[8,32,512]{2,1,0:T(8,128)(2,1)S(1)}, u32[]{:S(2)}, u32[]{:S(2)}) async-start(bf16[8,32,512]{2,1,0:T(8,128)(2,1)} %copy.24), calls=%async_computation | async-start | bytes 524288 | tf_op jit(solution)/shard_map/all_to_all | solution.py:36
  13.5 1.0 %copy-start = (bf16[256,512]{1,0:T(8,128)(2,1)S(1)}, bf16[256,512]{1,0:T(8,128)(2,1)}, u32[]{:S(2)}) copy-start(bf16[256,512]{1,0:T(8,128)(2,1)} %param.7) | copy-start | bytes 786436
  25.1 12.6 %copy-start.3 = (s32[1,2,2]{2,1,0:T(2,128)S(1)}, s32[1,2,2]{2,1,0:T(2,128)}, u32[]{:S(2)}) copy-start(s32[1,2,2]{2,1,0:T(2,128)} %param.9) | copy-start | bytes 52
  25.1 29.9 %all-to-all-start.1 = ((f32[64,16,128]{2,1,0:T(8,128)}), f32[64,16,128]{2,1,0:T(8,128)S(1)}, u32[]{:S(2)}, u32[]{:S(2)}) async-start(f32[64,16,128]{2,1,0:T(8,128)} %bitcast.8), calls=%async_computation.1 | async-start | bytes 1048576 | tf_op jit(solution)/shard_map/all_to_all | solution.py:44
  56.3 18.3 %all-to-all-start.2 = ((bf16[64,16,128]{2,1,0:T(8,128)(2,1)}), bf16[64,16,128]{2,1,0:T(8,128)(2,1)S(1)}, u32[]{:S(2)}, u32[]{:S(2)}) async-start(bf16[64,16,128]{2,1,0:T(8,128)(2,1)} %bitcast.55), calls=%async_computation.2 | async-start | bytes 524288 | tf_op jit(solution)/shard_map/all_to_all | solution.py:52

commit v4 on v0

--- a/solution.py
+++ b/solution.py
@@ -4,6 +4,8 @@
 import jax.numpy as jnp
 import numpy as np
 from jax import lax
+from jax.experimental import pallas as pl
+from jax.experimental.pallas import tpu as pltpu
 from jax.sharding import Mesh
 from jax.sharding import PartitionSpec as P
 
@@ -54,6 +56,37 @@
     return both[0], both[1]
 
 
+def finish_kernel(att_scale, intra_q, intra_k, intra_v, g, v, k_rows, state, adjoint, out_q, out_k, out_v):
+    f32 = jnp.float32
+    nt = (((1,), (1,)), ((), ()))
+    nn = (((1,), (0,)), ((), ()))
+    for h in range(state.shape[0]):
+        cols = pl.ds(h * HD, HD)
+        gh = g[:, cols]
+        vh = v[:, cols]
+        qg = lax.dot_general(gh, state[h], nt, preferred_element_type=f32)
+        kg = lax.dot_general(vh, adjoint[h], nt, preferred_element_type=f32)
+        vg = lax.dot_general(k_rows[h], adjoint[h], nn, preferred_element_type=f32)
+        out_q[:, cols] = (intra_q[h] + att_scale * qg).astype(out_q.dtype)
+        out_k[:, cols] = (intra_k[h] + att_scale * kg).astype(out_k.dtype)
+        out_v[:, cols] = (intra_v[h] + att_scale * vg).astype(out_v.dtype)
+
+
+def finish(att_scale, intra_q, intra_k, intra_v, g, v, k_rows, state, adjoint):
+    heads, rows, _ = intra_q.shape
+    shape = jax.ShapeDtypeStruct((rows, heads * HD), jnp.bfloat16)
+    flops = 3 * 2 * heads * rows * HD * HD
+    moved = 3 * heads * rows * HD * 4 + 3 * rows * heads * HD * 2 + 3 * rows * heads * HD * 2
+    return pl.pallas_call(
+        lambda *refs: finish_kernel(att_scale, *refs),
+        out_shape=(shape, shape, shape),
+        in_specs=[pl.BlockSpec(memory_space=pltpu.VMEM)] * 8,
+        out_specs=[pl.BlockSpec(memory_space=pltpu.VMEM)] * 3,
+        cost_estimate=pl.CostEstimate(flops=flops, bytes_accessed=moved, transcendentals=0),
+        name="finish_outputs",
+    )(intra_q, intra_k, intra_v, g, v, k_rows, state, adjoint)
+
+
 def make_local(sizes, n_head):
     n_ctx = sizes[0] * sizes[1] * sizes[2]
 
@@ -66,7 +99,8 @@
         q = unpack_bits(query_bits, head_group)
         k = unpack_bits(key_bits, head_group)
         v = values.reshape(tok_rows, head_group, HD)
-        g = gather_heads(grad_out, n_head, values.shape[1]).reshape(tok_rows, head_group, HD)
+        g2 = gather_heads(grad_out, n_head, values.shape[1])
+        g = g2.reshape(tok_rows, head_group, HD)
         state_term = jnp.einsum("hds,she->hde", k, v, preferred_element_type=f32)
         adj_term = jnp.einsum("hdt,the->hde", q, g, preferred_element_type=f32)
         state, adjoint = carried_sums(state_term, adj_term, n_ctx)
@@ -76,21 +110,11 @@
         grad_w = (att_scale * pair * keep).astype(bf16)
         spk = jnp.einsum("hdt,hds->hts", q, k, preferred_element_type=f32)
         att_w = (att_scale * spk * keep).astype(bf16)
-        query_grad = jnp.einsum("hts,hds->thd", grad_w, k, preferred_element_type=f32) + att_scale * jnp.einsum(
-            "the,hde->thd", g, state, preferred_element_type=f32
-        )
-        key_grad = jnp.einsum("hts,hdt->shd", grad_w, q, preferred_element_type=f32) + att_scale * jnp.einsum(
-            "she,hde->shd", v, adjoint, preferred_element_type=f32
-        )
-        value_grad = jnp.einsum("hts,the->she", att_w, g, preferred_element_type=f32) + att_scale * jnp.einsum(
-            "hds,hde->she", k, adjoint, preferred_element_type=f32
-        )
-        shape = (tok_rows, head_group * HD)
-        return (
-            query_grad.astype(bf16).reshape(shape),
-            key_grad.astype(bf16).reshape(shape),
-            value_grad.astype(bf16).reshape(shape),
-        )
+        intra_q = jnp.einsum("hts,hds->htd", grad_w, k, preferred_element_type=f32)
+        intra_k = jnp.einsum("hts,hdt->hsd", grad_w, q, preferred_element_type=f32)
+        intra_v = jnp.einsum("hts,the->hse", att_w, g, preferred_element_type=f32)
+        k_rows = jnp.swapaxes(k, 1, 2)
+        return finish(att_scale, intra_q, intra_k, intra_v, g2, values, k_rows, state, adjoint)
 
     return local
 

time: 78.9 us -> 79.2 us (level)
  waiting for transfers between devices: 37.5 us -> 32.6 us
  Pallas kernels: 0 us -> 2.87 us
  matrix products: 3.1 us -> 5 us
    pallas_call x0 -> x1, Pallas kernels: none -> 2.87 us  [finish(): pl.pallas_call(lambda *refs: finish_kernel(att_scale, *refs), out_shape=(...]
    all_to_all x1, waiting for transfers between devices: 9.98 us -> 8.13 us  [gather_heads(): got = lax.all_to_all(blocks, 'head', 0, 0, tiled=True)]
    dot_general x6 -> x3, matrix products: 1.78 us -> 3.6 us  [the longest x1 1.38 us: local(): intra_v = jnp.einsum('hts,the->hse', att_w, g, preferred_element_type=f32)]
    all_to_all x1, waiting for transfers between devices: 11.1 us -> 9.45 us  [carried_sums(): lax.all_to_all(sums.astype(jnp.bfloat16).reshape(n_ctx, -1, HD), CTX, 0,...]
    all_to_all x1, waiting for transfers between devices: 16.4 us -> 15 us  [carried_sums(): got = lax.all_to_all(terms, CTX, 0, 0, tiled=True)]
    unnamed x13 -> x14, local copies, waits for them, and re-layouts: 5.04 us -> 4.44 us
  transfers between devices with their start and end apart: 3 -> 3, of which waited for: 3 -> 3; matrix products, arithmetic and copies ran while one was open for 2% -> 6% of each run, Pallas kernels for 0% -> 0%
where the time goes in v4:
time: 79.2 us; the launch traced here: 78.7 us
  waiting for transfers between devices  32.6 us (41%)
  starting transfers between devices  29.7 us (38%)
  local copies, waits for them, and re-layouts  6.67 us (8%)
  matrix products  5 us (6%)
  Pallas kernels  2.87 us (4%)
  other arithmetic  1.01 us (1%)
    all_to_all x1, waiting for transfers between devices, carried_sums(): got = lax.all_to_all(terms, CTX, 0, 0, tiled=True)  15 us
    all_to_all x1, starting transfers between devices, carried_sums(): got = lax.all_to_all(terms, CTX, 0, 0, tiled=True)  12.5 us
    all_to_all x1, starting transfers between devices, gather_heads(): got = lax.all_to_all(blocks, 'head', 0, 0, tiled=True)  11 us
    all_to_all x1, waiting for transfers between devices, carried_sums(): lax.all_to_all(sums.astype(jnp.bfloat16).reshape(n_ctx, -1, HD), CTX, 0,...  9.45 us
    all_to_all x1, waiting for transfers between devices, gather_heads(): got = lax.all_to_all(blocks, 'head', 0, 0, tiled=True)  8.13 us
    all_to_all x1, starting transfers between devices, carried_sums(): lax.all_to_all(sums.astype(jnp.bfloat16).reshape(n_ctx, -1, HD), CTX, 0,...  6.29 us
    unnamed x14, local copies, waits for them, and re-layouts  4.44 us
    pallas_call x1, Pallas kernels, finish(): pl.pallas_call(lambda *refs: finish_kernel(att_scale, *refs), out_shape=(...  2.87 us
  transfers between devices with their start and end apart: 3, of which 3 were waited for; matrix products, arithmetic and copies ran while one was open for 6% of the time, Pallas kernels for 0%

profile of v4, /device:TPU:1, one launch (start us, length us, event | category | flops | bytes accessed | tf_op | source)
XLA Modules:
  0.0 78.7 jit_solution(6132940975774968574)
XLA Ops:
  0.6 1.0 %copy.40 = bf16[4,8,8,512]{3,2,1,0:T(8,128)(2,1)S(1)} copy(bf16[4,8,8,512]{3,1,2,0:T(8,128)(2,1)} %bitcast.59) | data formatting | bytes 524288
  1.7 0.8 copy.64
  2.5 11.0 %all-to-all-start = ((bf16[8,32,512]{2,1,0:T(8,128)(2,1)}), bf16[8,32,512]{2,1,0:T(8,128)(2,1)S(1)}, u32[]{:S(2)}, u32[]{:S(2)}) async-start(bf16[8,32,512]{2,1,0:T(8,128)(2,1)} %bitcast.49), calls=%async_computation | async-start | bytes 524288 | tf_op jit(solution)/shard_map/all_to_all | solution.py:38
  13.7 0.6 copy-done.4
  14.3 0.2 copy.24
  14.7 0.8 %copy-done.1 = bf16[256,512]{1,0:T(8,128)(2,1)S(1)} copy-done((bf16[256,512]{1,0:T(8,128)(2,1)S(1)}, bf16[256,512]{1,0:T(8,128)(2,1)}, u32[]{:S(2)}) %copy-start.1) | copy-done | bytes 262168
  15.5 0.3 fusion.8
  15.8 8.1 %all-to-all-done = bf16[8,32,512]{2,1,0:T(8,128)(2,1)S(1)} async-done(((bf16[8,32,512]{2,1,0:T(8,128)(2,1)}), bf16[8,32,512]{2,1,0:T(8,128)(2,1)S(1)}, u32[]{:S(2)}, u32[]{:S(2)}) %all-to-all-start) | async-done | bytes 262176 | tf_op jit(solution)/shard_map/all_to_all | solution.py:38
  24.0 0.6 copy-done.2
  24.6 0.3 fusion.13
  24.9 0.8 %pad_maximum_fusion = f32[8,128,128]{2,1,0:T(8,128)} fusion(f32[4,128,128]{2,1,0:T(8,128)S(1)} %fusion.13, f32[4,128,128]{2,1,0:T(8,128)S(1)} %fusion.8), kind=kLoop, calls=%fused_computation.9 | loop fusion | flops 131072 | bytes 1048576 | tf_op jit(solution)/shard_map/concatenate | solution.py:45
  25.7 12.5 %all-to-all-start.1 = ((f32[64,16,128]{2,1,0:T(8,128)}), f32[64,16,128]{2,1,0:T(8,128)S(1)}, u32[]{:S(2)}, u32[]{:S(2)}) async-start(f32[64,16,128]{2,1,0:T(8,128)} %bitcast.8), calls=%async_computation.1 | async-start | bytes 1048576 | tf_op jit(solution)/shard_map/all_to_all | solution.py:46
  38.2 0.7 copy-done.5
  39.1 0.3 fusion
  39.4 1.1 %fusion.21.refs_0_ = f32[4,256,128]{2,1,0:T(8,128)} fusion(bf16[4,256,256]{2,1,0:T(8,128)(2,1)S(1)} %fusion, bf16[4,128,256]{1,2,0:T(8,128)(2,1)S(1)} %get-tuple-element.6), kind=kOutput, calls=%fused_computation.33 | convolution fusion | flops 67108864 | bytes 1310720 | tf_op jit(solution)/shard_map/hts,hds->htd/dot_general | solution.py:113
  40.5 15.0 %all-to-all-done.1 = f32[64,16,128]{2,1,0:T(8,128)S(1)} async-done(((f32[64,16,128]{2,1,0:T(8,128)}), f32[64,16,128]{2,1,0:T(8,128)S(1)}, u32[]{:S(2)}, u32[]{:S(2)}) %all-to-all-start.1) | async-done | bytes 524320 | tf_op jit(solution)/shard_map/all_to_all | solution.py:46
  55.5 0.6 fusion.3
  56.1 0.7 copy.43
  56.8 6.3 %all-to-all-start.2 = ((bf16[64,16,128]{2,1,0:T(8,128)(2,1)}), bf16[64,16,128]{2,1,0:T(8,128)(2,1)S(1)}, u32[]{:S(2)}, u32[]{:S(2)}) async-start(bf16[64,16,128]{2,1,0:T(8,128)(2,1)} %bitcast.22), calls=%async_computation.2 | async-start | bytes 524288 | tf_op jit(solution)/shard_map/all_to_all | solution.py:54
  63.1 1.1 %fusion.22.refs_1_ = f32[4,256,128]{2,1,0:T(8,128)} fusion(bf16[4,256,256]{2,1,0:T(8,128)(2,1)S(1)} %fusion, bf16[4,128,256]{1,2,0:T(8,128)(2,1)S(1)} %get-tuple-element.5), kind=kOutput, calls=%fused_computation.34 | convolution fusion | flops 67108864 | bytes 1310720 | tf_op jit(solution)/shard_map/hts,hdt->hsd/dot_general | solution.py:114
  64.2 1.4 %fusion.2.refs_2_ = f32[4,256,128]{2,1,0:T(8,128)} fusion(bf16[4,128,256]{1,2,0:T(8,128)(2,1)S(1)} %get-tuple-element.5, bf16[4,128,256]{1,2,0:T(8,128)(2,1)S(1)} %get-tuple-element.6, f32[256,256]{1,0:T(8,128)S(1)} %fusion.7, bf16[256,4,128]{2,1,0:T(4,128)(2,1)S(1)} %reshape_reshape.3), kind=kOutput, calls=%fused_computation.5 | convolution fusion | flops 134742016 | bytes 1572864 | tf_op jit(solution)/shard_map/hts,the->hse/dot_general | solution.py:115
  65.6 9.4 %all-to-all-done.2 = bf16[64,16,128]{2,1,0:T(8,128)(2,1)S(1)} async-done(((bf16[64,16,128]{2,1,0:T(8,128)(2,1)}), bf16[64,16,128]{2,1,0:T(8,128)(2,1)S(1)}, u32[]{:S(2)}, u32[]{:S(2)}) %all-to-all-start.2) | async-done | bytes 262176 | tf_op jit(solution)/shard_map/all_to_all | solution.py:54
  75.1 0.7 fusion.20
  75.8 2.9 %finish_outputs.1 = (bf16[256,512]{1,0:T(8,128)(2,1)}, bf16[256,512]{1,0:T(8,128)(2,1)}, bf16[256,512]{1,0:T(8,128)(2,1)}) custom-call(f32[4,256,128]{2,1,0:T(8,128)} %fusion.21.refs_0_, f32[4,256,128]{2,1,0:T(8,128)} %fusion.22.refs_1_, f32[4,256,128]{2,1,0:T(8,128)} %fusion.2.refs_2_, bf16[256,512]{1,0:T(8,128)(2,1)} %bitcast.51, ...), custom_call_target="tpu_custom_call" | custom-call | flops 100663296 | bytes 3145728 | tf_op jit(solution)/shard_map/finish_outputs/pallas_call | solution.py:80
  (18 shorter events, 0.7 us)
Async XLA Ops:
  2.4 11.0 %copy-start.3 = (s32[32,256]{1,0:T(8,128)S(1)}, s32[32,256]{1,0:T(8,128)}, u32[]{:S(2)}) copy-start(s32[32,256]{1,0:T(8,128)} %param.6) | copy-start | bytes 98308
  2.5 21.5 %all-to-all-start = ((bf16[8,32,512]{2,1,0:T(8,128)(2,1)}), bf16[8,32,512]{2,1,0:T(8,128)(2,1)S(1)}, u32[]{:S(2)}, u32[]{:S(2)}) async-start(bf16[8,32,512]{2,1,0:T(8,128)(2,1)} %bitcast.49), calls=%async_computation | async-start | bytes 524288 | tf_op jit(solution)/shard_map/all_to_all | solution.py:38
  13.5 0.8 copy-start.4
  14.6 1.0 %copy-start.1 = (bf16[256,512]{1,0:T(8,128)(2,1)S(1)}, bf16[256,512]{1,0:T(8,128)(2,1)}, u32[]{:S(2)}) copy-start(bf16[256,512]{1,0:T(8,128)(2,1)} %refs_4_.1) | copy-start | bytes 786436
  14.7 49.5 %copy-start = (bf16[4,128,256]{1,2,0:T(8,128)(2,1)}, bf16[4,128,256]{1,2,0:T(8,128)(2,1)S(1)}, u32[]{:S(2)}) copy-start(bf16[4,128,256]{1,2,0:T(8,128)(2,1)S(1)} %get-tuple-element.6) | copy-start | bytes 786436
  23.9 0.7 copy-start.2
  25.7 29.7 %all-to-all-start.1 = ((f32[64,16,128]{2,1,0:T(8,128)}), f32[64,16,128]{2,1,0:T(8,128)S(1)}, u32[]{:S(2)}, u32[]{:S(2)}) async-start(f32[64,16,128]{2,1,0:T(8,128)} %bitcast.8), calls=%async_computation.1 | async-start | bytes 1048576 | tf_op jit(solution)/shard_map/all_to_all | solution.py:46
  38.2 0.7 copy-start.5
  56.8 18.3 %all-to-all-start.2 = ((bf16[64,16,128]{2,1,0:T(8,128)(2,1)}), bf16[64,16,128]{2,1,0:T(8,128)(2,1)S(1)}, u32[]{:S(2)}, u32[]{:S(2)}) async-start(bf16[64,16,128]{2,1,0:T(8,128)(2,1)} %bitcast.22), calls=%async_computation.2 | async-start | bytes 524288 | tf_op jit(solution)/shard_map/all_to_all | solution.py:54

commit v5 on v4

--- a/solution.py
+++ b/solution.py
@@ -34,8 +34,8 @@
 
 def gather_heads(grad_out, n_head, width):
     tok_part = grad_out.shape[1]
-    blocks = grad_out[0].reshape(tok_part, n_head, width).transpose(1, 0, 2)
-    got = lax.all_to_all(blocks, "head", 0, 0, tiled=True)
+    blocks = grad_out[0].reshape(tok_part, n_head, width)
+    got = lax.all_to_all(blocks, "head", 1, 0, tiled=True)
     return got.reshape(n_head * tok_part, width)
 
 
@@ -48,31 +48,30 @@
     row = jnp.arange(n_ctx, dtype=jnp.int32)[:, None]
     col = jnp.arange(n_ctx, dtype=jnp.int32)[None, :]
     mix = jnp.where(me < n_ctx // 2, col < row, col > row).astype(f32)
-    sums = jnp.dot(
-        mix, got.reshape(n_ctx, -1), precision=lax.Precision.HIGHEST, preferred_element_type=f32
+    sums = jnp.einsum(
+        "ij,jrc->irc", mix, got, precision=lax.Precision.HIGHEST, preferred_element_type=f32
     )
-    back = lax.all_to_all(sums.astype(jnp.bfloat16).reshape(n_ctx, -1, HD), CTX, 0, 0, tiled=True)
-    both = back.reshape(2, heads, HD, HD)
-    return both[0], both[1]
+    back = lax.all_to_all(sums.astype(jnp.bfloat16), CTX, 0, 0, tiled=True)
+    return back.reshape(2, heads, HD, HD)
 
 
-def finish_kernel(att_scale, intra_q, intra_k, intra_v, g, v, k_rows, state, adjoint, out_q, out_k, out_v):
+def finish_kernel(att_scale, intra_q, intra_k, intra_v, g, v, k_rows, carried, out_q, out_k, out_v):
     f32 = jnp.float32
     nt = (((1,), (1,)), ((), ()))
     nn = (((1,), (0,)), ((), ()))
-    for h in range(state.shape[0]):
+    for h in range(carried.shape[1]):
         cols = pl.ds(h * HD, HD)
         gh = g[:, cols]
         vh = v[:, cols]
-        qg = lax.dot_general(gh, state[h], nt, preferred_element_type=f32)
-        kg = lax.dot_general(vh, adjoint[h], nt, preferred_element_type=f32)
-        vg = lax.dot_general(k_rows[h], adjoint[h], nn, preferred_element_type=f32)
+        qg = lax.dot_general(gh, carried[0, h], nt, preferred_element_type=f32)
+        kg = lax.dot_general(vh, carried[1, h], nt, preferred_element_type=f32)
+        vg = lax.dot_general(k_rows[h], carried[1, h], nn, preferred_element_type=f32)
         out_q[:, cols] = (intra_q[h] + att_scale * qg).astype(out_q.dtype)
         out_k[:, cols] = (intra_k[h] + att_scale * kg).astype(out_k.dtype)
         out_v[:, cols] = (intra_v[h] + att_scale * vg).astype(out_v.dtype)
 
 
-def finish(att_scale, intra_q, intra_k, intra_v, g, v, k_rows, state, adjoint):
+def finish(att_scale, intra_q, intra_k, intra_v, g, v, k_rows, carried):
     heads, rows, _ = intra_q.shape
     shape = jax.ShapeDtypeStruct((rows, heads * HD), jnp.bfloat16)
     flops = 3 * 2 * heads * rows * HD * HD
@@ -80,11 +79,11 @@
     return pl.pallas_call(
         lambda *refs: finish_kernel(att_scale, *refs),
         out_shape=(shape, shape, shape),
-        in_specs=[pl.BlockSpec(memory_space=pltpu.VMEM)] * 8,
+        in_specs=[pl.BlockSpec(memory_space=pltpu.VMEM)] * 7,
         out_specs=[pl.BlockSpec(memory_space=pltpu.VMEM)] * 3,
         cost_estimate=pl.CostEstimate(flops=flops, bytes_accessed=moved, transcendentals=0),
         name="finish_outputs",
-    )(intra_q, intra_k, intra_v, g, v, k_rows, state, adjoint)
+    )(intra_q, intra_k, intra_v, g, v, k_rows, carried)
 
 
 def make_local(sizes, n_head):
@@ -103,7 +102,7 @@
         g = g2.reshape(tok_rows, head_group, HD)
         state_term = jnp.einsum("hds,she->hde", k, v, preferred_element_type=f32)
         adj_term = jnp.einsum("hdt,the->hde", q, g, preferred_element_type=f32)
-        state, adjoint = carried_sums(state_term, adj_term, n_ctx)
+        carried = carried_sums(state_term, adj_term, n_ctx)
 
         keep = token_mask(tile_mask[0], tok_rows // tile_mask.shape[1])
         pair = jnp.einsum("the,she->hts", g, v, preferred_element_type=f32)
@@ -114,7 +113,7 @@
         intra_k = jnp.einsum("hts,hdt->hsd", grad_w, q, preferred_element_type=f32)
         intra_v = jnp.einsum("hts,the->hse", att_w, g, preferred_element_type=f32)
         k_rows = jnp.swapaxes(k, 1, 2)
-        return finish(att_scale, intra_q, intra_k, intra_v, g2, values, k_rows, state, adjoint)
+        return finish(att_scale, intra_q, intra_k, intra_v, g2, values, k_rows, carried)
 
     return local
 

time: 79.2 us -> 79.3 us (level)
    convert_element_type x0 -> x1, local copies, waits for them, and re-layouts: none -> 0.88 us  [carried_sums(): back = lax.all_to_all(sums.astype(jnp.bfloat16), CTX, 0, 0, tiled=True)]
    unnamed x14 -> x15, local copies, waits for them, and re-layouts: 4.44 us -> 4.39 us
where the time goes in v5:
time: 79.3 us; the launch traced here: 78.8 us
  waiting for transfers between devices  32.6 us (41%)
  starting transfers between devices  29.7 us (37%)
  local copies, waits for them, and re-layouts  6.78 us (9%)
  matrix products  5 us (6%)
  Pallas kernels  2.87 us (4%)
  other arithmetic  1.01 us (1%)
    all_to_all x1, waiting for transfers between devices, carried_sums(): got = lax.all_to_all(terms, CTX, 0, 0, tiled=True)  15 us
    all_to_all x1, starting transfers between devices, carried_sums(): got = lax.all_to_all(terms, CTX, 0, 0, tiled=True)  12.5 us
    all_to_all x1, starting transfers between devices, gather_heads(): got = lax.all_to_all(blocks, 'head', 1, 0, tiled=True)  11 us
    all_to_all x1, waiting for transfers between devices, carried_sums(): back = lax.all_to_all(sums.astype(jnp.bfloat16), CTX, 0, 0, tiled=True)  9.45 us
    all_to_all x1, waiting for transfers between devices, gather_heads(): got = lax.all_to_all(blocks, 'head', 1, 0, tiled=True)  8.13 us
    all_to_all x1, starting transfers between devices, carried_sums(): back = lax.all_to_all(sums.astype(jnp.bfloat16), CTX, 0, 0, tiled=True)  6.29 us
    unnamed x15, local copies, waits for them, and re-layouts  4.39 us
    pallas_call x1, Pallas kernels, finish(): pl.pallas_call(lambda *refs: finish_kernel(att_scale, *refs), out_shape=(...  2.87 us
  transfers between devices with their start and end apart: 3, of which 3 were waited for; matrix products, arithmetic and copies ran while one was open for 6% of the time, Pallas kernels for 0%

profile of v5, /device:TPU:1, one launch (start us, length us, event | category | flops | bytes accessed | tf_op | source)
XLA Modules:
  0.0 78.8 jit_solution(3072296717888823894)
XLA Ops:
  0.6 1.0 %copy.62 = bf16[4,8,8,512]{3,2,1,0:T(8,128)(2,1)S(1)} copy(bf16[4,8,8,512]{3,1,2,0:T(8,128)(2,1)} %bitcast.58) | data formatting | bytes 524288
  1.7 0.8 copy.37
  2.5 11.0 %all-to-all-start = ((bf16[32,8,512]{2,0,1:T(8,128)(2,1)}), bf16[32,8,512]{2,0,1:T(8,128)(2,1)S(1)}, u32[]{:S(2)}, u32[]{:S(2)}) async-start(bf16[32,8,512]{2,0,1:T(8,128)(2,1)} %copy.37), calls=%async_computation | async-start | bytes 524288 | tf_op jit(solution)/shard_map/all_to_all | solution.py:38
  13.7 0.6 copy-done.5
  14.3 0.2 copy.42
  14.7 0.8 %copy-done.1 = bf16[256,512]{1,0:T(8,128)(2,1)S(1)} copy-done((bf16[256,512]{1,0:T(8,128)(2,1)S(1)}, bf16[256,512]{1,0:T(8,128)(2,1)}, u32[]{:S(2)}) %copy-start.1) | copy-done | bytes 262168
  15.5 0.3 fusion.6
  15.8 8.1 %all-to-all-done = bf16[32,8,512]{2,0,1:T(8,128)(2,1)S(1)} async-done(((bf16[32,8,512]{2,0,1:T(8,128)(2,1)}), bf16[32,8,512]{2,0,1:T(8,128)(2,1)S(1)}, u32[]{:S(2)}, u32[]{:S(2)}) %all-to-all-start) | async-done | bytes 262176 | tf_op jit(solution)/shard_map/all_to_all | solution.py:38
  24.0 0.6 copy-done.2
  24.6 0.3 fusion.11
  24.9 0.8 %pad_maximum_fusion = f32[8,128,128]{2,1,0:T(8,128)} fusion(f32[4,128,128]{2,1,0:T(8,128)S(1)} %fusion.11, f32[4,128,128]{2,1,0:T(8,128)S(1)} %fusion.6), kind=kLoop, calls=%fused_computation.6 | loop fusion | flops 131072 | bytes 1048576 | tf_op jit(solution)/shard_map/concatenate | solution.py:45
  25.7 12.5 %all-to-all-start.1 = ((f32[64,16,128]{2,1,0:T(8,128)}), f32[64,16,128]{2,1,0:T(8,128)S(1)}, u32[]{:S(2)}, u32[]{:S(2)}) async-start(f32[64,16,128]{2,1,0:T(8,128)} %bitcast.11), calls=%async_computation.1 | async-start | bytes 1048576 | tf_op jit(solution)/shard_map/all_to_all | solution.py:46
  38.2 0.7 copy-done.6
  39.1 0.3 fusion
  39.4 1.1 %fusion.19.refs_0_ = f32[4,256,128]{2,1,0:T(8,128)} fusion(bf16[4,256,256]{2,1,0:T(8,128)(2,1)S(1)} %fusion, bf16[4,128,256]{1,2,0:T(8,128)(2,1)S(1)} %get-tuple-element.4), kind=kOutput, calls=%fused_computation.30 | convolution fusion | flops 67108864 | bytes 1310720 | tf_op jit(solution)/shard_map/hts,hds->htd/dot_general | solution.py:112
  40.5 15.0 %all-to-all-done.1 = f32[64,16,128]{2,1,0:T(8,128)S(1)} async-done(((f32[64,16,128]{2,1,0:T(8,128)}), f32[64,16,128]{2,1,0:T(8,128)S(1)}, u32[]{:S(2)}, u32[]{:S(2)}) %all-to-all-start.1) | async-done | bytes 524320 | tf_op jit(solution)/shard_map/all_to_all | solution.py:46
  55.5 0.6 convolution_convert_fusion
  56.1 0.9 %copy.53 = bf16[64,16,128]{2,1,0:T(8,128)(2,1)} copy(bf16[64,16,128]{2,0,1:T(8,128)(2,1)S(1)} %convolution_convert_fusion) | data formatting | bytes 524288 | tf_op jit(solution)/shard_map/convert_element_type | solution.py:54
  56.9 6.3 %all-to-all-start.2 = ((bf16[64,16,128]{2,1,0:T(8,128)(2,1)}), bf16[64,16,128]{2,1,0:T(8,128)(2,1)S(1)}, u32[]{:S(2)}, u32[]{:S(2)}) async-start(bf16[64,16,128]{2,1,0:T(8,128)(2,1)} %copy.53), calls=%async_computation.2 | async-start | bytes 524288 | tf_op jit(solution)/shard_map/all_to_all | solution.py:54
  63.2 1.1 %fusion.20.refs_1_ = f32[4,256,128]{2,1,0:T(8,128)} fusion(bf16[4,256,256]{2,1,0:T(8,128)(2,1)S(1)} %fusion, bf16[4,128,256]{1,2,0:T(8,128)(2,1)S(1)} %get-tuple-element.3), kind=kOutput, calls=%fused_computation.31 | convolution fusion | flops 67108864 | bytes 1310720 | tf_op jit(solution)/shard_map/hts,hdt->hsd/dot_general | solution.py:113
  64.4 1.4 %fusion.2.refs_2_ = f32[4,256,128]{2,1,0:T(8,128)} fusion(bf16[4,128,256]{1,2,0:T(8,128)(2,1)S(1)} %get-tuple-element.3, bf16[4,128,256]{1,2,0:T(8,128)(2,1)S(1)} %get-tuple-element.4, f32[256,256]{1,0:T(8,128)S(1)} %fusion.5, bf16[256,4,128]{2,1,0:T(4,128)(2,1)S(1)} %reshape_reshape.3), kind=kOutput, calls=%fused_computation.4 | convolution fusion | flops 134742016 | bytes 1572864 | tf_op jit(solution)/shard_map/hts,the->hse/dot_general | solution.py:114
  65.8 9.4 %all-to-all-done.2 = bf16[64,16,128]{2,1,0:T(8,128)(2,1)S(1)} async-done(((bf16[64,16,128]{2,1,0:T(8,128)(2,1)}), bf16[64,16,128]{2,1,0:T(8,128)(2,1)S(1)}, u32[]{:S(2)}, u32[]{:S(2)}) %all-to-all-start.2) | async-done | bytes 262176 | tf_op jit(solution)/shard_map/all_to_all | solution.py:54
  75.2 0.7 copy-done.3
  75.9 2.9 %finish_outputs.1 = (bf16[256,512]{1,0:T(8,128)(2,1)}, bf16[256,512]{1,0:T(8,128)(2,1)}, bf16[256,512]{1,0:T(8,128)(2,1)}) custom-call(f32[4,256,128]{2,1,0:T(8,128)} %fusion.19.refs_0_, f32[4,256,128]{2,1,0:T(8,128)} %fusion.20.refs_1_, f32[4,256,128]{2,1,0:T(8,128)} %fusion.2.refs_2_, bf16[256,512]{1,0:T(8,128)(2,1)} %bitcast.52, ...), custom_call_target="tpu_custom_call" | custom-call | flops 100663296 | bytes 3145728 | tf_op jit(solution)/shard_map/finish_outputs/pallas_call | solution.py:79
  (19 shorter events, 0.7 us)
Async XLA Ops:
  2.4 11.0 %copy-start.4 = (s32[32,256]{1,0:T(8,128)S(1)}, s32[32,256]{1,0:T(8,128)}, u32[]{:S(2)}) copy-start(s32[32,256]{1,0:T(8,128)} %param.6) | copy-start | bytes 98308
  2.5 21.5 %all-to-all-start = ((bf16[32,8,512]{2,0,1:T(8,128)(2,1)}), bf16[32,8,512]{2,0,1:T(8,128)(2,1)S(1)}, u32[]{:S(2)}, u32[]{:S(2)}) async-start(bf16[32,8,512]{2,0,1:T(8,128)(2,1)} %copy.37), calls=%async_computation | async-start | bytes 524288 | tf_op jit(solution)/shard_map/all_to_all | solution.py:38
  13.5 0.8 copy-start.5
  14.6 1.0 %copy-start.1 = (bf16[256,512]{1,0:T(8,128)(2,1)S(1)}, bf16[256,512]{1,0:T(8,128)(2,1)}, u32[]{:S(2)}) copy-start(bf16[256,512]{1,0:T(8,128)(2,1)} %refs_4_.1) | copy-start | bytes 786436
  14.7 49.6 %copy-start = (bf16[4,128,256]{1,2,0:T(8,128)(2,1)}, bf16[4,128,256]{1,2,0:T(8,128)(2,1)S(1)}, u32[]{:S(2)}) copy-start(bf16[4,128,256]{1,2,0:T(8,128)(2,1)S(1)} %get-tuple-element.4) | copy-start | bytes 786436
  23.9 0.7 copy-start.2
  25.7 29.7 %all-to-all-start.1 = ((f32[64,16,128]{2,1,0:T(8,128)}), f32[64,16,128]{2,1,0:T(8,128)S(1)}, u32[]{:S(2)}, u32[]{:S(2)}) async-start(f32[64,16,128]{2,1,0:T(8,128)} %bitcast.11), calls=%async_computation.1 | async-start | bytes 1048576 | tf_op jit(solution)/shard_map/all_to_all | solution.py:46
  38.2 0.7 copy-start.6
  56.9 18.3 %all-to-all-start.2 = ((bf16[64,16,128]{2,1,0:T(8,128)(2,1)}), bf16[64,16,128]{2,1,0:T(8,128)(2,1)S(1)}, u32[]{:S(2)}, u32[]{:S(2)}) async-start(bf16[64,16,128]{2,1,0:T(8,128)(2,1)} %copy.53), calls=%async_computation.2 | async-start | bytes 524288 | tf_op jit(solution)/shard_map/all_to_all | solution.py:54
  75.2 0.7 copy-start.3

commit v6 on v5

--- a/solution.py
+++ b/solution.py
@@ -59,16 +59,12 @@
     f32 = jnp.float32
     nt = (((1,), (1,)), ((), ()))
     nn = (((1,), (0,)), ((), ()))
-    for h in range(carried.shape[1]):
-        cols = pl.ds(h * HD, HD)
-        gh = g[:, cols]
-        vh = v[:, cols]
-        qg = lax.dot_general(gh, carried[0, h], nt, preferred_element_type=f32)
-        kg = lax.dot_general(vh, carried[1, h], nt, preferred_element_type=f32)
-        vg = lax.dot_general(k_rows[h], carried[1, h], nn, preferred_element_type=f32)
-        out_q[:, cols] = (intra_q[h] + att_scale * qg).astype(out_q.dtype)
-        out_k[:, cols] = (intra_k[h] + att_scale * kg).astype(out_k.dtype)
-        out_v[:, cols] = (intra_v[h] + att_scale * vg).astype(out_v.dtype)
+    qg = lax.dot_general(g[...], carried[0, 0], nt, preferred_element_type=f32)
+    kg = lax.dot_general(v[...], carried[1, 0], nt, preferred_element_type=f32)
+    vg = lax.dot_general(k_rows[0], carried[1, 0], nn, preferred_element_type=f32)
+    out_q[...] = (intra_q[0] + att_scale * qg).astype(out_q.dtype)
+    out_k[...] = (intra_k[0] + att_scale * kg).astype(out_k.dtype)
+    out_v[...] = (intra_v[0] + att_scale * vg).astype(out_v.dtype)
 
 
 def finish(att_scale, intra_q, intra_k, intra_v, g, v, k_rows, carried):
@@ -76,11 +72,22 @@
     shape = jax.ShapeDtypeStruct((rows, heads * HD), jnp.bfloat16)
     flops = 3 * 2 * heads * rows * HD * HD
     moved = 3 * heads * rows * HD * 4 + 3 * rows * heads * HD * 2 + 3 * rows * heads * HD * 2
+    per_head = pl.BlockSpec((1, rows, HD), lambda h: (h, 0, 0))
+    columns = pl.BlockSpec((rows, HD), lambda h: (0, h))
     return pl.pallas_call(
         lambda *refs: finish_kernel(att_scale, *refs),
         out_shape=(shape, shape, shape),
-        in_specs=[pl.BlockSpec(memory_space=pltpu.VMEM)] * 7,
-        out_specs=[pl.BlockSpec(memory_space=pltpu.VMEM)] * 3,
+        grid=(heads,),
+        in_specs=[
+            per_head,
+            per_head,
+            per_head,
+            columns,
+            columns,
+            per_head,
+            pl.BlockSpec((2, 1, HD, HD), lambda h: (0, h, 0, 0)),
+        ],
+        out_specs=[columns, columns, columns],
         cost_estimate=pl.CostEstimate(flops=flops, bytes_accessed=moved, transcendentals=0),
         name="finish_outputs",
     )(intra_q, intra_k, intra_v, g, v, k_rows, carried)

time: 79.3 us -> 80.5 us (1.015)
  Pallas kernels: 2.87 us -> 3.96 us
    pallas_call x1, Pallas kernels: 2.87 us -> 3.96 us  [finish(): pl.pallas_call(lambda *refs: finish_kernel(att_scale, *refs), out_shape=(...]
where the time goes in v6:
time: 80.5 us; the launch traced here: 79.9 us
  waiting for transfers between devices  32.6 us (40%)
  starting transfers between devices  29.7 us (37%)
  local copies, waits for them, and re-layouts  6.78 us (8%)
  matrix products  5 us (6%)
  Pallas kernels  3.96 us (5%)
  other arithmetic  1.01 us (1%)
    all_to_all x1, waiting for transfers between devices, carried_sums(): got = lax.all_to_all(terms, CTX, 0, 0, tiled=True)  15 us
    all_to_all x1, starting transfers between devices, carried_sums(): got = lax.all_to_all(terms, CTX, 0, 0, tiled=True)  12.5 us
    all_to_all x1, starting transfers between devices, gather_heads(): got = lax.all_to_all(blocks, 'head', 1, 0, tiled=True)  11 us
    all_to_all x1, waiting for transfers between devices, carried_sums(): back = lax.all_to_all(sums.astype(jnp.bfloat16), CTX, 0, 0, tiled=True)  9.45 us
    all_to_all x1, waiting for transfers between devices, gather_heads(): got = lax.all_to_all(blocks, 'head', 1, 0, tiled=True)  8.13 us
    all_to_all x1, starting transfers between devices, carried_sums(): back = lax.all_to_all(sums.astype(jnp.bfloat16), CTX, 0, 0, tiled=True)  6.29 us
    unnamed x15, local copies, waits for them, and re-layouts  4.39 us
    pallas_call x1, Pallas kernels, finish(): pl.pallas_call(lambda *refs: finish_kernel(att_scale, *refs), out_shape=(...  3.96 us
  transfers between devices with their start and end apart: 3, of which 3 were waited for; matrix products, arithmetic and copies ran while one was open for 6% of the time, Pallas kernels for 0%

profile of v6, /device:TPU:1, one launch (start us, length us, event | category | flops | bytes accessed | tf_op | source)
XLA Modules:
  0.0 79.9 jit_solution(3890576296181345596)
XLA Ops:
  0.6 1.0 %copy.62 = bf16[4,8,8,512]{3,2,1,0:T(8,128)(2,1)S(1)} copy(bf16[4,8,8,512]{3,1,2,0:T(8,128)(2,1)} %bitcast.58) | data formatting | bytes 524288
  1.7 0.8 copy.37
  2.5 11.0 %all-to-all-start = ((bf16[32,8,512]{2,0,1:T(8,128)(2,1)}), bf16[32,8,512]{2,0,1:T(8,128)(2,1)S(1)}, u32[]{:S(2)}, u32[]{:S(2)}) async-start(bf16[32,8,512]{2,0,1:T(8,128)(2,1)} %copy.37), calls=%async_computation | async-start | bytes 524288 | tf_op jit(solution)/shard_map/all_to_all | solution.py:38
  13.7 0.6 copy-done.5
  14.3 0.2 copy.42
  14.7 0.8 copy-done.1
  15.5 0.3 fusion.6
  15.8 8.1 %all-to-all-done = bf16[32,8,512]{2,0,1:T(8,128)(2,1)S(1)} async-done(((bf16[32,8,512]{2,0,1:T(8,128)(2,1)}), bf16[32,8,512]{2,0,1:T(8,128)(2,1)S(1)}, u32[]{:S(2)}, u32[]{:S(2)}) %all-to-all-start) | async-done | bytes 262176 | tf_op jit(solution)/shard_map/all_to_all | solution.py:38
  24.0 0.6 copy-done.2
  24.6 0.3 fusion.11
  24.9 0.8 %pad_maximum_fusion = f32[8,128,128]{2,1,0:T(8,128)} fusion(f32[4,128,128]{2,1,0:T(8,128)S(1)} %fusion.11, f32[4,128,128]{2,1,0:T(8,128)S(1)} %fusion.6), kind=kLoop, calls=%fused_computation.6 | loop fusion | flops 131072 | bytes 1048576 | tf_op jit(solution)/shard_map/concatenate | solution.py:45
  25.7 12.5 %all-to-all-start.1 = ((f32[64,16,128]{2,1,0:T(8,128)}), f32[64,16,128]{2,1,0:T(8,128)S(1)}, u32[]{:S(2)}, u32[]{:S(2)}) async-start(f32[64,16,128]{2,1,0:T(8,128)} %bitcast.11), calls=%async_computation.1 | async-start | bytes 1048576 | tf_op jit(solution)/shard_map/all_to_all | solution.py:46
  38.2 0.7 copy-done.6
  39.1 0.3 fusion
  39.4 1.1 %fusion.19.refs_0_ = f32[4,256,128]{2,1,0:T(8,128)} fusion(bf16[4,256,256]{2,1,0:T(8,128)(2,1)S(1)} %fusion, bf16[4,128,256]{1,2,0:T(8,128)(2,1)S(1)} %get-tuple-element.4), kind=kOutput, calls=%fused_computation.30 | convolution fusion | flops 67108864 | bytes 1310720 | tf_op jit(solution)/shard_map/hts,hds->htd/dot_general | solution.py:119
  40.5 15.0 %all-to-all-done.1 = f32[64,16,128]{2,1,0:T(8,128)S(1)} async-done(((f32[64,16,128]{2,1,0:T(8,128)}), f32[64,16,128]{2,1,0:T(8,128)S(1)}, u32[]{:S(2)}, u32[]{:S(2)}) %all-to-all-start.1) | async-done | bytes 524320 | tf_op jit(solution)/shard_map/all_to_all | solution.py:46
  55.5 0.6 convolution_convert_fusion
  56.1 0.9 %copy.53 = bf16[64,16,128]{2,1,0:T(8,128)(2,1)} copy(bf16[64,16,128]{2,0,1:T(8,128)(2,1)S(1)} %convolution_convert_fusion) | data formatting | bytes 524288 | tf_op jit(solution)/shard_map/convert_element_type | solution.py:54
  56.9 6.3 %all-to-all-start.2 = ((bf16[64,16,128]{2,1,0:T(8,128)(2,1)}), bf16[64,16,128]{2,1,0:T(8,128)(2,1)S(1)}, u32[]{:S(2)}, u32[]{:S(2)}) async-start(bf16[64,16,128]{2,1,0:T(8,128)(2,1)} %copy.53), calls=%async_computation.2 | async-start | bytes 524288 | tf_op jit(solution)/shard_map/all_to_all | solution.py:54
  63.2 1.1 %fusion.20.refs_1_ = f32[4,256,128]{2,1,0:T(8,128)} fusion(bf16[4,256,256]{2,1,0:T(8,128)(2,1)S(1)} %fusion, bf16[4,128,256]{1,2,0:T(8,128)(2,1)S(1)} %get-tuple-element.3), kind=kOutput, calls=%fused_computation.31 | convolution fusion | flops 67108864 | bytes 1310720 | tf_op jit(solution)/shard_map/hts,hdt->hsd/dot_general | solution.py:120
  64.4 1.4 %fusion.2.refs_2_ = f32[4,256,128]{2,1,0:T(8,128)} fusion(bf16[4,128,256]{1,2,0:T(8,128)(2,1)S(1)} %get-tuple-element.3, bf16[4,128,256]{1,2,0:T(8,128)(2,1)S(1)} %get-tuple-element.4, f32[256,256]{1,0:T(8,128)S(1)} %fusion.5, bf16[256,4,128]{2,1,0:T(4,128)(2,1)S(1)} %reshape_reshape.3), kind=kOutput, calls=%fused_computation.4 | convolution fusion | flops 134742016 | bytes 1572864 | tf_op jit(solution)/shard_map/hts,the->hse/dot_general | solution.py:121
  65.8 9.4 %all-to-all-done.2 = bf16[64,16,128]{2,1,0:T(8,128)(2,1)S(1)} async-done(((bf16[64,16,128]{2,1,0:T(8,128)(2,1)}), bf16[64,16,128]{2,1,0:T(8,128)(2,1)S(1)}, u32[]{:S(2)}, u32[]{:S(2)}) %all-to-all-start.2) | async-done | bytes 262176 | tf_op jit(solution)/shard_map/all_to_all | solution.py:54
  75.2 0.7 copy-done.3
  75.9 4.0 %finish_outputs.1 = (bf16[256,512]{1,0:T(8,128)(2,1)}, bf16[256,512]{1,0:T(8,128)(2,1)}, bf16[256,512]{1,0:T(8,128)(2,1)}) custom-call(f32[4,256,128]{2,1,0:T(8,128)} %fusion.19.refs_0_, f32[4,256,128]{2,1,0:T(8,128)} %fusion.20.refs_1_, f32[4,256,128]{2,1,0:T(8,128)} %fusion.2.refs_2_, bf16[256,512]{1,0:T(8,128)(2,1)} %bitcast.52, ...), custom_call_target="tpu_custom_call" | custom-call | flops 100663296 | bytes 3145728 | tf_op jit(solution)/shard_map/finish_outputs/pallas_call | solution.py:77
  (19 shorter events, 0.7 us)
Async XLA Ops:
  2.4 11.0 %copy-start.4 = (s32[32,256]{1,0:T(8,128)S(1)}, s32[32,256]{1,0:T(8,128)}, u32[]{:S(2)}) copy-start(s32[32,256]{1,0:T(8,128)} %param.6) | copy-start | bytes 98308
  2.5 21.5 %all-to-all-start = ((bf16[32,8,512]{2,0,1:T(8,128)(2,1)}), bf16[32,8,512]{2,0,1:T(8,128)(2,1)S(1)}, u32[]{:S(2)}, u32[]{:S(2)}) async-start(bf16[32,8,512]{2,0,1:T(8,128)(2,1)} %copy.37), calls=%async_computation | async-start | bytes 524288 | tf_op jit(solution)/shard_map/all_to_all | solution.py:38
  13.5 0.8 copy-start.5
  14.6 1.0 %copy-start.1 = (bf16[256,512]{1,0:T(8,128)(2,1)S(1)}, bf16[256,512]{1,0:T(8,128)(2,1)}, u32[]{:S(2)}) copy-start(bf16[256,512]{1,0:T(8,128)(2,1)} %refs_4_.1) | copy-start | bytes 786436
  14.7 49.6 %copy-start = (bf16[4,128,256]{1,2,0:T(8,128)(2,1)}, bf16[4,128,256]{1,2,0:T(8,128)(2,1)S(1)}, u32[]{:S(2)}) copy-start(bf16[4,128,256]{1,2,0:T(8,128)(2,1)S(1)} %get-tuple-element.4) | copy-start | bytes 786436
  23.9 0.7 copy-start.2
  25.7 29.7 %all-to-all-start.1 = ((f32[64,16,128]{2,1,0:T(8,128)}), f32[64,16,128]{2,1,0:T(8,128)S(1)}, u32[]{:S(2)}, u32[]{:S(2)}) async-start(f32[64,16,128]{2,1,0:T(8,128)} %bitcast.11), calls=%async_computation.1 | async-start | bytes 1048576 | tf_op jit(solution)/shard_map/all_to_all | solution.py:46
  38.2 0.7 copy-start.6
  56.9 18.3 %all-to-all-start.2 = ((bf16[64,16,128]{2,1,0:T(8,128)(2,1)}), bf16[64,16,128]{2,1,0:T(8,128)(2,1)S(1)}, u32[]{:S(2)}, u32[]{:S(2)}) async-start(bf16[64,16,128]{2,1,0:T(8,128)(2,1)} %copy.53), calls=%async_computation.2 | async-start | bytes 524288 | tf_op jit(solution)/shard_map/all_to_all | solution.py:54
  75.2 0.7 copy-start.3

commit v7 on v5

--- a/solution.py
+++ b/solution.py
@@ -39,19 +39,35 @@
     return got.reshape(n_head * tok_part, width)
 
 
+def running_kernel(flag, got, out):
+    n = got.shape[0]
+    reverse = flag[0]
+
+    def step(i, acc):
+        at = jnp.where(reverse == 1, n - 1 - i, i)
+        out[at] = acc.astype(out.dtype)
+        return acc + got[at]
+
+    lax.fori_loop(0, n, step, jnp.zeros(got.shape[1:], jnp.float32), unroll=8)
+
+
+def running_sums(flag, got):
+    return pl.pallas_call(
+        running_kernel,
+        out_shape=jax.ShapeDtypeStruct(got.shape, jnp.bfloat16),
+        in_specs=[pl.BlockSpec(memory_space=pltpu.SMEM), pl.BlockSpec(memory_space=pltpu.VMEM)],
+        out_specs=pl.BlockSpec(memory_space=pltpu.VMEM),
+        name="running_sums",
+    )(flag, got)
+
+
 def carried_sums(state_term, adj_term, n_ctx):
-    f32 = jnp.float32
     heads = state_term.shape[0]
     terms = jnp.concatenate([state_term, adj_term], axis=0).reshape(n_ctx, -1, HD)
     got = lax.all_to_all(terms, CTX, 0, 0, tiled=True)
     me = lax.axis_index(CTX)
-    row = jnp.arange(n_ctx, dtype=jnp.int32)[:, None]
-    col = jnp.arange(n_ctx, dtype=jnp.int32)[None, :]
-    mix = jnp.where(me < n_ctx // 2, col < row, col > row).astype(f32)
-    sums = jnp.einsum(
-        "ij,jrc->irc", mix, got, precision=lax.Precision.HIGHEST, preferred_element_type=f32
-    )
-    back = lax.all_to_all(sums.astype(jnp.bfloat16), CTX, 0, 0, tiled=True)
+    flag = jnp.where(me < n_ctx // 2, 0, 1).astype(jnp.int32).reshape(1)
+    back = lax.all_to_all(running_sums(flag, got), CTX, 0, 0, tiled=True)
     return back.reshape(2, heads, HD, HD)
 
 

time: 79.3 us -> 80.7 us (1.018)
  Pallas kernels: 2.87 us -> 4.77 us
    pallas_call x0 -> x1, Pallas kernels: none -> 1.9 us  [running_sums(): pl.pallas_call(running_kernel, out_shape=jax.ShapeDtypeStruct(got.shape,...]
    convert_element_type x1 -> x0, local copies, waits for them, and re-layouts: 0.88 us -> none  [carried_sums(): back = lax.all_to_all(sums.astype(jnp.bfloat16), CTX, 0, 0, tiled=True)]
    unnamed x15 -> x17, local copies, waits for them, and re-layouts: 4.39 us -> 5.22 us
where the time goes in v7:
time: 80.7 us; the launch traced here: 80.1 us
  waiting for transfers between devices  32.6 us (40%)
  starting transfers between devices  29.7 us (37%)
  local copies, waits for them, and re-layouts  6.74 us (8%)
  Pallas kernels  4.77 us (6%)
  matrix products  4.45 us (6%)
  other arithmetic  1.02 us (1%)
    all_to_all x1, waiting for transfers between devices, carried_sums(): got = lax.all_to_all(terms, CTX, 0, 0, tiled=True)  15 us
    all_to_all x1, starting transfers between devices, carried_sums(): got = lax.all_to_all(terms, CTX, 0, 0, tiled=True)  12.4 us
    all_to_all x1, starting transfers between devices, gather_heads(): got = lax.all_to_all(blocks, 'head', 1, 0, tiled=True)  11 us
    all_to_all x1, waiting for transfers between devices, carried_sums(): back = lax.all_to_all(running_sums(flag, got), CTX, 0, 0, tiled=True)  9.43 us
    all_to_all x1, waiting for transfers between devices, gather_heads(): got = lax.all_to_all(blocks, 'head', 1, 0, tiled=True)  8.13 us
    all_to_all x1, starting transfers between devices, carried_sums(): back = lax.all_to_all(running_sums(flag, got), CTX, 0, 0, tiled=True)  6.29 us
    unnamed x17, local copies, waits for them, and re-layouts  5.22 us
    pallas_call x1, Pallas kernels, finish(): pl.pallas_call(lambda *refs: finish_kernel(att_scale, *refs), out_shape=(...  2.87 us
  transfers between devices with their start and end apart: 3, of which 3 were waited for; matrix products, arithmetic and copies ran while one was open for 6% of the time, Pallas kernels for 0%

profile of v7, /device:TPU:1, one launch (start us, length us, event | category | flops | bytes accessed | tf_op | source)
XLA Modules:
  0.0 80.1 jit_solution(18403979866636700112)
XLA Ops:
  0.6 1.0 %copy.40 = bf16[4,8,8,512]{3,2,1,0:T(8,128)(2,1)S(1)} copy(bf16[4,8,8,512]{3,1,2,0:T(8,128)(2,1)} %bitcast.56) | data formatting | bytes 524288
  1.7 0.8 copy.19
  2.5 11.0 %all-to-all-start = ((bf16[32,8,512]{2,0,1:T(8,128)(2,1)}), bf16[32,8,512]{2,0,1:T(8,128)(2,1)S(1)}, u32[]{:S(2)}, u32[]{:S(2)}) async-start(bf16[32,8,512]{2,0,1:T(8,128)(2,1)} %copy.19), calls=%async_computation | async-start | bytes 524288 | tf_op jit(solution)/shard_map/all_to_all | solution.py:38
  13.5 0.2 copy.22
  13.7 0.6 copy-done.6
  14.7 0.8 copy-done.1
  15.5 0.3 fusion.5
  15.8 8.1 %all-to-all-done = bf16[32,8,512]{2,0,1:T(8,128)(2,1)S(1)} async-done(((bf16[32,8,512]{2,0,1:T(8,128)(2,1)}), bf16[32,8,512]{2,0,1:T(8,128)(2,1)S(1)}, u32[]{:S(2)}, u32[]{:S(2)}) %all-to-all-start) | async-done | bytes 262176 | tf_op jit(solution)/shard_map/all_to_all | solution.py:38
  24.0 0.6 copy-done.2
  24.6 0.3 fusion.10
  24.9 0.8 %pad_maximum_fusion = f32[8,128,128]{2,1,0:T(8,128)} fusion(f32[4,128,128]{2,1,0:T(8,128)S(1)} %fusion.10, f32[4,128,128]{2,1,0:T(8,128)S(1)} %fusion.5), kind=kLoop, calls=%fused_computation.5 | loop fusion | flops 131072 | bytes 1048576 | tf_op jit(solution)/shard_map/concatenate | solution.py:66
  25.8 12.4 %all-to-all-start.1 = ((f32[64,16,128]{2,1,0:T(8,128)}), f32[64,16,128]{2,1,0:T(8,128)S(1)}, u32[]{:S(2)}, u32[]{:S(2)}) async-start(f32[64,16,128]{2,1,0:T(8,128)} %bitcast.11), calls=%async_computation.1 | async-start | bytes 1048576 | tf_op jit(solution)/shard_map/all_to_all | solution.py:67
  38.3 0.7 copy-done.7
  39.1 0.3 fusion
  39.4 1.1 %fusion.14.refs_0_ = f32[4,256,128]{2,1,0:T(8,128)} fusion(bf16[4,256,256]{2,1,0:T(8,128)(2,1)S(1)} %fusion, bf16[4,128,256]{1,2,0:T(8,128)(2,1)S(1)} %get-tuple-element.4), kind=kOutput, calls=%fused_computation.23 | convolution fusion | flops 67108864 | bytes 1310720 | tf_op jit(solution)/shard_map/hts,hds->htd/dot_general | solution.py:128
  40.5 15.0 %all-to-all-done.1.got = f32[64,16,128]{2,1,0:T(8,128)S(1)} async-done(((f32[64,16,128]{2,1,0:T(8,128)}), f32[64,16,128]{2,1,0:T(8,128)S(1)}, u32[]{:S(2)}, u32[]{:S(2)}) %all-to-all-start.1) | async-done | bytes 524320 | tf_op jit(solution)/shard_map/all_to_all | solution.py:67
  55.5 0.8 %copy-done.3 = f32[64,16,128]{2,1,0:T(8,128)} copy-done((f32[64,16,128]{2,1,0:T(8,128)}, f32[64,16,128]{2,1,0:T(8,128)S(1)}, u32[]{:S(2)}) %copy-start.3) | copy-done | bytes 524312
  56.3 1.9 %running_sums.1 = bf16[64,16,128]{2,1,0:T(8,128)(2,1)} custom-call(s32[1]{0:T(128)} %bitcast.10.flag, f32[64,16,128]{2,1,0:T(8,128)} %copy-done.3), custom_call_target="tpu_custom_call" | custom-call | tf_op jit(solution)/shard_map/running_sums/pallas_call | solution.py:55
  58.2 6.3 %all-to-all-start.2 = ((bf16[64,16,128]{2,1,0:T(8,128)(2,1)}), bf16[64,16,128]{2,1,0:T(8,128)(2,1)S(1)}, u32[]{:S(2)}, u32[]{:S(2)}) async-start(bf16[64,16,128]{2,1,0:T(8,128)(2,1)} %running_sums.1), calls=%async_computation.2 | async-start | bytes 524288 | tf_op jit(solution)/shard_map/all_to_all | solution.py:70
  64.5 1.2 %fusion.15.refs_1_ = f32[4,256,128]{2,1,0:T(8,128)} fusion(bf16[4,256,256]{2,1,0:T(8,128)(2,1)S(1)} %fusion, bf16[4,128,256]{1,2,0:T(8,128)(2,1)S(1)} %get-tuple-element.3), kind=kOutput, calls=%fused_computation.24 | convolution fusion | flops 67108864 | bytes 1310720 | tf_op jit(solution)/shard_map/hts,hdt->hsd/dot_general | solution.py:129
  65.7 1.4 %fusion.2.refs_2_ = f32[4,256,128]{2,1,0:T(8,128)} fusion(bf16[4,128,256]{1,2,0:T(8,128)(2,1)S(1)} %get-tuple-element.3, bf16[4,128,256]{1,2,0:T(8,128)(2,1)S(1)} %get-tuple-element.4, f32[256,256]{1,0:T(8,128)S(1)} %fusion.4, bf16[256,4,128]{2,1,0:T(4,128)(2,1)S(1)} %reshape_reshape.3), kind=kOutput, calls=%fused_computation.4 | convolution fusion | flops 134742016 | bytes 1572864 | tf_op jit(solution)/shard_map/hts,the->hse/dot_general | solution.py:130
  67.1 9.4 %all-to-all-done.2 = bf16[64,16,128]{2,1,0:T(8,128)(2,1)S(1)} async-done(((bf16[64,16,128]{2,1,0:T(8,128)(2,1)}), bf16[64,16,128]{2,1,0:T(8,128)(2,1)S(1)}, u32[]{:S(2)}, u32[]{:S(2)}) %all-to-all-start.2) | async-done | bytes 262176 | tf_op jit(solution)/shard_map/all_to_all | solution.py:70
  76.5 0.7 copy-done.4
  77.2 2.9 %finish_outputs.1 = (bf16[256,512]{1,0:T(8,128)(2,1)}, bf16[256,512]{1,0:T(8,128)(2,1)}, bf16[256,512]{1,0:T(8,128)(2,1)}) custom-call(f32[4,256,128]{2,1,0:T(8,128)} %fusion.14.refs_0_, f32[4,256,128]{2,1,0:T(8,128)} %fusion.15.refs_1_, f32[4,256,128]{2,1,0:T(8,128)} %fusion.2.refs_2_, bf16[256,512]{1,0:T(8,128)(2,1)} %bitcast.50, ...), custom_call_target="tpu_custom_call" | custom-call | flops 100663296 | bytes 3145728 | tf_op jit(solution)/shard_map/finish_outputs/pallas_call | solution.py:95
  (20 shorter events, 0.7 us)
Async XLA Ops:
  2.4 11.0 %copy-start.5 = (s32[32,256]{1,0:T(8,128)S(1)}, s32[32,256]{1,0:T(8,128)}, u32[]{:S(2)}) copy-start(s32[32,256]{1,0:T(8,128)} %param.6) | copy-start | bytes 98308
  2.5 21.5 %all-to-all-start = ((bf16[32,8,512]{2,0,1:T(8,128)(2,1)}), bf16[32,8,512]{2,0,1:T(8,128)(2,1)S(1)}, u32[]{:S(2)}, u32[]{:S(2)}) async-start(bf16[32,8,512]{2,0,1:T(8,128)(2,1)} %copy.19), calls=%async_computation | async-start | bytes 524288 | tf_op jit(solution)/shard_map/all_to_all | solution.py:38
  13.5 0.8 copy-start.6
  14.6 1.0 %copy-start.1 = (bf16[256,512]{1,0:T(8,128)(2,1)S(1)}, bf16[256,512]{1,0:T(8,128)(2,1)}, u32[]{:S(2)}) copy-start(bf16[256,512]{1,0:T(8,128)(2,1)} %refs_4_.1) | copy-start | bytes 786436
  14.7 50.9 %copy-start = (bf16[4,128,256]{1,2,0:T(8,128)(2,1)}, bf16[4,128,256]{1,2,0:T(8,128)(2,1)S(1)}, u32[]{:S(2)}) copy-start(bf16[4,128,256]{1,2,0:T(8,128)(2,1)S(1)} %get-tuple-element.4) | copy-start | bytes 786436
  23.9 0.7 copy-start.2
  25.8 29.7 %all-to-all-start.1 = ((f32[64,16,128]{2,1,0:T(8,128)}), f32[64,16,128]{2,1,0:T(8,128)S(1)}, u32[]{:S(2)}, u32[]{:S(2)}) async-start(f32[64,16,128]{2,1,0:T(8,128)} %bitcast.11), calls=%async_computation.1 | async-start | bytes 1048576 | tf_op jit(solution)/shard_map/all_to_all | solution.py:67
  38.2 0.7 copy-start.7
  55.5 0.8 %copy-start.3 = (f32[64,16,128]{2,1,0:T(8,128)}, f32[64,16,128]{2,1,0:T(8,128)S(1)}, u32[]{:S(2)}) copy-start(f32[64,16,128]{2,1,0:T(8,128)S(1)} %all-to-all-done.1.got) | copy-start | bytes 1572868
  58.2 18.3 %all-to-all-start.2 = ((bf16[64,16,128]{2,1,0:T(8,128)(2,1)}), bf16[64,16,128]{2,1,0:T(8,128)(2,1)S(1)}, u32[]{:S(2)}, u32[]{:S(2)}) async-start(bf16[64,16,128]{2,1,0:T(8,128)(2,1)} %running_sums.1), calls=%async_computation.2 | async-start | bytes 524288 | tf_op jit(solution)/shard_map/all_to_all | solution.py:70
  76.5 0.7 copy-start.4

commit v8 on v0

--- a/solution.py
+++ b/solution.py
@@ -32,7 +32,9 @@
 
 def gather_heads(grad_out, n_head, width):
     tok_part = grad_out.shape[1]
-    blocks = grad_out[0].reshape(tok_part, n_head, width).transpose(1, 0, 2)
+    blocks = jnp.concatenate(
+        [grad_out[0, :, j * width : (j + 1) * width] for j in range(n_head)], axis=0
+    ).reshape(n_head, tok_part, width)
     got = lax.all_to_all(blocks, "head", 0, 0, tiled=True)
     return got.reshape(n_head * tok_part, width)
 

time: 78.9 us -> 88.5 us (1.12)
  local copies, waits for them, and re-layouts: 6.3 us -> 15.5 us
    unnamed x13 -> x19, local copies, waits for them, and re-layouts: 5.04 us -> 13.6 us
    concatenate x0 -> x1, local copies, waits for them, and re-layouts: none -> 1.37 us  [gather_heads(): jnp.concatenate([grad_out[0, :, j * width:(j + 1) * width] for j in range...]
where the time goes in v8:
time: 88.5 us; the launch traced here: 87.6 us
  waiting for transfers between devices  37.5 us (42%)
  starting transfers between devices  29.7 us (34%)
  local copies, waits for them, and re-layouts  15.5 us (18%)
  matrix products  3.1 us (4%)
  other arithmetic  1.06 us (1%)
    all_to_all x1, waiting for transfers between devices, carried_sums(): got = lax.all_to_all(terms, CTX, 0, 0, tiled=True)  16.4 us
    unnamed x19, local copies, waits for them, and re-layouts  13.6 us
    all_to_all x1, starting transfers between devices, carried_sums(): got = lax.all_to_all(terms, CTX, 0, 0, tiled=True)  12.5 us
    all_to_all x1, waiting for transfers between devices, carried_sums(): lax.all_to_all(sums.astype(jnp.bfloat16).reshape(n_ctx, -1, HD), CTX, 0,...  11.1 us
    all_to_all x1, starting transfers between devices, gather_heads(): got = lax.all_to_all(blocks, 'head', 0, 0, tiled=True)  11 us
    all_to_all x1, waiting for transfers between devices, gather_heads(): got = lax.all_to_all(blocks, 'head', 0, 0, tiled=True)  9.98 us
    all_to_all x1, starting transfers between devices, carried_sums(): lax.all_to_all(sums.astype(jnp.bfloat16).reshape(n_ctx, -1, HD), CTX, 0,...  6.29 us
  transfers between devices with their start and end apart: 3, of which 3 were waited for; matrix products, arithmetic and copies ran while one was open for 2% of the time, Pallas kernels for 0%

profile of v8, /device:TPU:1, one launch (start us, length us, event | category | flops | bytes accessed | tf_op | source)
XLA Modules:
  0.0 87.6 jit_solution(5352444826740694534)
XLA Ops:
  0.6 1.4 %bitcast_dynamic-update-slice_fusion.7 = bf16[256,512]{1,0:T(8,128)(2,1)} fusion(bf16[1,32,4096]{2,1,0:T(8,128)(2,1)} %param.8), kind=kLoop, calls=%fused_computation.43 | loop fusion | bytes 65536
  2.1 1.4 %bitcast_dynamic-update-slice_fusion.6 = bf16[256,512]{1,0:T(8,128)(2,1)} fusion(bf16[256,512]{1,0:T(8,128)(2,1)} %bitcast_dynamic-update-slice_fusion.7, bf16[1,32,4096]{2,1,0:T(8,128)(2,1)} %param.8), kind=kLoop, calls=%fused_computation.42 | loop fusion | bytes 65536
  3.4 1.4 %bitcast_dynamic-update-slice_fusion.5 = bf16[256,512]{1,0:T(8,128)(2,1)} fusion(bf16[256,512]{1,0:T(8,128)(2,1)} %bitcast_dynamic-update-slice_fusion.6, bf16[1,32,4096]{2,1,0:T(8,128)(2,1)} %param.8), kind=kLoop, calls=%fused_computation.41 | loop fusion | bytes 65536
  4.8 1.4 %bitcast_dynamic-update-slice_fusion.4 = bf16[256,512]{1,0:T(8,128)(2,1)} fusion(bf16[256,512]{1,0:T(8,128)(2,1)} %bitcast_dynamic-update-slice_fusion.5, bf16[1,32,4096]{2,1,0:T(8,128)(2,1)} %param.8), kind=kLoop, calls=%fused_computation.40 | loop fusion | bytes 65536
  6.2 1.4 %bitcast_dynamic-update-slice_fusion.3 = bf16[256,512]{1,0:T(8,128)(2,1)} fusion(bf16[256,512]{1,0:T(8,128)(2,1)} %bitcast_dynamic-update-slice_fusion.4, bf16[1,32,4096]{2,1,0:T(8,128)(2,1)} %param.8), kind=kLoop, calls=%fused_computation.39 | loop fusion | bytes 65536
  7.6 1.4 %bitcast_dynamic-update-slice_fusion.2 = bf16[256,512]{1,0:T(8,128)(2,1)} fusion(bf16[256,512]{1,0:T(8,128)(2,1)} %bitcast_dynamic-update-slice_fusion.3, bf16[1,32,4096]{2,1,0:T(8,128)(2,1)} %param.8), kind=kLoop, calls=%fused_computation.38 | loop fusion | bytes 65536
  8.9 1.4 %bitcast_dynamic-update-slice_fusion.1 = bf16[256,512]{1,0:T(8,128)(2,1)} fusion(bf16[256,512]{1,0:T(8,128)(2,1)} %bitcast_dynamic-update-slice_fusion.2, bf16[1,32,4096]{2,1,0:T(8,128)(2,1)} %param.8), kind=kLoop, calls=%fused_computation.37 | loop fusion | bytes 65536
  10.3 1.4 %bitcast_dynamic-update-slice_fusion = bf16[256,512]{1,0:T(8,128)(2,1)} fusion(bf16[256,512]{1,0:T(8,128)(2,1)} %bitcast_dynamic-update-slice_fusion.1, bf16[1,32,4096]{2,1,0:T(8,128)(2,1)} %param.8), kind=kLoop, calls=%fused_computation.36 | loop fusion | bytes 65536 | tf_op jit(solution)/shard_map/concatenate | solution.py:35
  11.7 11.0 %all-to-all-start = ((bf16[8,32,512]{2,1,0:T(8,128)(2,1)}), bf16[8,32,512]{2,1,0:T(8,128)(2,1)S(1)}, u32[]{:S(2)}, u32[]{:S(2)}) async-start(bf16[8,32,512]{2,1,0:T(8,128)(2,1)} %bitcast.10), calls=%async_computation | async-start | bytes 524288 | tf_op jit(solution)/shard_map/all_to_all | solution.py:38
  23.2 10.0 %all-to-all-done = bf16[8,32,512]{2,1,0:T(8,128)(2,1)S(1)} async-done(((bf16[8,32,512]{2,1,0:T(8,128)(2,1)}), bf16[8,32,512]{2,1,0:T(8,128)(2,1)S(1)}, u32[]{:S(2)}, u32[]{:S(2)}) %all-to-all-start) | async-done | bytes 262176 | tf_op jit(solution)/shard_map/all_to_all | solution.py:38
  33.6 0.8 pad_maximum_fusion
  34.5 12.5 %all-to-all-start.1 = ((f32[64,16,128]{2,1,0:T(8,128)}), f32[64,16,128]{2,1,0:T(8,128)S(1)}, u32[]{:S(2)}, u32[]{:S(2)}) async-start(f32[64,16,128]{2,1,0:T(8,128)} %bitcast.14), calls=%async_computation.1 | async-start | bytes 1048576 | tf_op jit(solution)/shard_map/all_to_all | solution.py:46
  47.0 0.7 copy-done.3
  47.8 16.4 %all-to-all-done.1 = f32[64,16,128]{2,1,0:T(8,128)S(1)} async-done(((f32[64,16,128]{2,1,0:T(8,128)}), f32[64,16,128]{2,1,0:T(8,128)S(1)}, u32[]{:S(2)}, u32[]{:S(2)}) %all-to-all-start.1) | async-done | bytes 524320 | tf_op jit(solution)/shard_map/all_to_all | solution.py:46
  64.2 0.6 fusion.9
  64.8 0.7 copy.31
  65.5 6.3 %all-to-all-start.2 = ((bf16[64,16,128]{2,1,0:T(8,128)(2,1)}), bf16[64,16,128]{2,1,0:T(8,128)(2,1)S(1)}, u32[]{:S(2)}, u32[]{:S(2)}) async-start(bf16[64,16,128]{2,1,0:T(8,128)(2,1)} %bitcast.34), calls=%async_computation.2 | async-start | bytes 524288 | tf_op jit(solution)/shard_map/all_to_all | solution.py:54
  71.8 0.3 fusion
  72.2 0.3 fusion.29
  72.7 11.1 %all-to-all-done.2 = bf16[64,16,128]{2,1,0:T(8,128)(2,1)S(1)} async-done(((bf16[64,16,128]{2,1,0:T(8,128)(2,1)}), bf16[64,16,128]{2,1,0:T(8,128)(2,1)S(1)}, u32[]{:S(2)}, u32[]{:S(2)}) %all-to-all-start.2) | async-done | bytes 262176 | tf_op jit(solution)/shard_map/all_to_all | solution.py:54
  84.1 0.5 fusion.8
  84.6 0.8 copy.26
  85.7 0.8 copy.24
  86.8 0.8 copy.25
  (22 shorter events, 2.1 us)
Async XLA Ops:
  0.6 22.3 %copy-start = (bf16[256,512]{1,0:T(8,128)(2,1)S(1)}, bf16[256,512]{1,0:T(8,128)(2,1)}, u32[]{:S(2)}) copy-start(bf16[256,512]{1,0:T(8,128)(2,1)} %param.7) | copy-start | bytes 786436
  11.7 11.1 %copy-start.1 = (s32[32,256]{1,0:T(8,128)S(1)}, s32[32,256]{1,0:T(8,128)}, u32[]{:S(2)}) copy-start(s32[32,256]{1,0:T(8,128)} %param.5) | copy-start | bytes 98308
  11.7 11.1 %copy-start.2 = (s32[32,256]{1,0:T(8,128)S(1)}, s32[32,256]{1,0:T(8,128)}, u32[]{:S(2)}) copy-start(s32[32,256]{1,0:T(8,128)} %param.6) | copy-start | bytes 98308
  11.7 21.5 %all-to-all-start = ((bf16[8,32,512]{2,1,0:T(8,128)(2,1)}), bf16[8,32,512]{2,1,0:T(8,128)(2,1)S(1)}, u32[]{:S(2)}, u32[]{:S(2)}) async-start(bf16[8,32,512]{2,1,0:T(8,128)(2,1)} %bitcast.10), calls=%async_computation | async-start | bytes 524288 | tf_op jit(solution)/shard_map/all_to_all | solution.py:38
  34.5 29.8 %all-to-all-start.1 = ((f32[64,16,128]{2,1,0:T(8,128)}), f32[64,16,128]{2,1,0:T(8,128)S(1)}, u32[]{:S(2)}, u32[]{:S(2)}) async-start(f32[64,16,128]{2,1,0:T(8,128)} %bitcast.14), calls=%async_computation.1 | async-start | bytes 1048576 | tf_op jit(solution)/shard_map/all_to_all | solution.py:46
  47.0 0.7 copy-start.3
  65.5 18.3 %all-to-all-start.2 = ((bf16[64,16,128]{2,1,0:T(8,128)(2,1)}), bf16[64,16,128]{2,1,0:T(8,128)(2,1)S(1)}, u32[]{:S(2)}, u32[]{:S(2)}) async-start(bf16[64,16,128]{2,1,0:T(8,128)(2,1)} %bitcast.34), calls=%async_computation.2 | async-start | bytes 524288 | tf_op jit(solution)/shard_map/all_to_all | solution.py:54

commit v9 on v5

--- a/solution.py
+++ b/solution.py
@@ -66,16 +66,16 @@
         qg = lax.dot_general(gh, carried[0, h], nt, preferred_element_type=f32)
         kg = lax.dot_general(vh, carried[1, h], nt, preferred_element_type=f32)
         vg = lax.dot_general(k_rows[h], carried[1, h], nn, preferred_element_type=f32)
-        out_q[:, cols] = (intra_q[h] + att_scale * qg).astype(out_q.dtype)
-        out_k[:, cols] = (intra_k[h] + att_scale * kg).astype(out_k.dtype)
-        out_v[:, cols] = (intra_v[h] + att_scale * vg).astype(out_v.dtype)
+        out_q[:, cols] = (intra_q[h].astype(f32) + att_scale * qg).astype(out_q.dtype)
+        out_k[:, cols] = (intra_k[h].astype(f32) + att_scale * kg).astype(out_k.dtype)
+        out_v[:, cols] = (intra_v[h].astype(f32) + att_scale * vg).astype(out_v.dtype)
 
 
 def finish(att_scale, intra_q, intra_k, intra_v, g, v, k_rows, carried):
     heads, rows, _ = intra_q.shape
     shape = jax.ShapeDtypeStruct((rows, heads * HD), jnp.bfloat16)
     flops = 3 * 2 * heads * rows * HD * HD
-    moved = 3 * heads * rows * HD * 4 + 3 * rows * heads * HD * 2 + 3 * rows * heads * HD * 2
+    moved = 3 * heads * rows * HD * 2 + 3 * rows * heads * HD * 2 + 3 * rows * heads * HD * 2
     return pl.pallas_call(
         lambda *refs: finish_kernel(att_scale, *refs),
         out_shape=(shape, shape, shape),
@@ -113,7 +113,16 @@
         intra_k = jnp.einsum("hts,hdt->hsd", grad_w, q, preferred_element_type=f32)
         intra_v = jnp.einsum("hts,the->hse", att_w, g, preferred_element_type=f32)
         k_rows = jnp.swapaxes(k, 1, 2)
-        return finish(att_scale, intra_q, intra_k, intra_v, g2, values, k_rows, carried)
+        return finish(
+            att_scale,
+            intra_q.astype(bf16),
+            intra_k.astype(bf16),
+            intra_v.astype(bf16),
+            g2,
+            values,
+            k_rows,
+            carried,
+        )
 
     return local
 

time: 79.3 us -> 79.1 us (level)
    all_to_all x1, waiting for transfers between devices: 15 us -> 16.1 us  [carried_sums(): got = lax.all_to_all(terms, CTX, 0, 0, tiled=True)]
where the time goes in v9:
time: 79.1 us; the launch traced here: 78.5 us
  waiting for transfers between devices  32.9 us (42%)
  starting transfers between devices  29.7 us (38%)
  local copies, waits for them, and re-layouts  6.79 us (9%)
  matrix products  4.69 us (6%)
  Pallas kernels  2.64 us (3%)
  other arithmetic  1.02 us (1%)
    all_to_all x1, waiting for transfers between devices, carried_sums(): got = lax.all_to_all(terms, CTX, 0, 0, tiled=True)  16.1 us
    all_to_all x1, starting transfers between devices, carried_sums(): got = lax.all_to_all(terms, CTX, 0, 0, tiled=True)  12.5 us
    all_to_all x1, starting transfers between devices, gather_heads(): got = lax.all_to_all(blocks, 'head', 1, 0, tiled=True)  11 us
    all_to_all x1, waiting for transfers between devices, carried_sums(): back = lax.all_to_all(sums.astype(jnp.bfloat16), CTX, 0, 0, tiled=True)  8.67 us
    all_to_all x1, waiting for transfers between devices, gather_heads(): got = lax.all_to_all(blocks, 'head', 1, 0, tiled=True)  8.13 us
    all_to_all x1, starting transfers between devices, carried_sums(): back = lax.all_to_all(sums.astype(jnp.bfloat16), CTX, 0, 0, tiled=True)  6.29 us
    unnamed x15, local copies, waits for them, and re-layouts  4.39 us
    pallas_call x1, Pallas kernels, finish(): pl.pallas_call(lambda *refs: finish_kernel(att_scale, *refs), out_shape=(...  2.64 us
  transfers between devices with their start and end apart: 3, of which 3 were waited for; matrix products, arithmetic and copies ran while one was open for 6% of the time, Pallas kernels for 0%

profile of v9, /device:TPU:1, one launch (start us, length us, event | category | flops | bytes accessed | tf_op | source)
XLA Modules:
  0.0 78.5 jit_solution(14598660494031272167)
XLA Ops:
  0.6 1.0 %copy.62 = bf16[4,8,8,512]{3,2,1,0:T(8,128)(2,1)S(1)} copy(bf16[4,8,8,512]{3,1,2,0:T(8,128)(2,1)} %bitcast.58) | data formatting | bytes 524288
  1.7 0.8 copy.37
  2.5 11.0 %all-to-all-start = ((bf16[32,8,512]{2,0,1:T(8,128)(2,1)}), bf16[32,8,512]{2,0,1:T(8,128)(2,1)S(1)}, u32[]{:S(2)}, u32[]{:S(2)}) async-start(bf16[32,8,512]{2,0,1:T(8,128)(2,1)} %copy.37), calls=%async_computation | async-start | bytes 524288 | tf_op jit(solution)/shard_map/all_to_all | solution.py:38
  13.7 0.6 copy-done.5
  14.3 0.2 copy.42
  14.7 0.8 %copy-done.1 = bf16[256,512]{1,0:T(8,128)(2,1)S(1)} copy-done((bf16[256,512]{1,0:T(8,128)(2,1)S(1)}, bf16[256,512]{1,0:T(8,128)(2,1)}, u32[]{:S(2)}) %copy-start.1) | copy-done | bytes 262168
  15.5 0.3 fusion.7
  15.8 8.1 %all-to-all-done = bf16[32,8,512]{2,0,1:T(8,128)(2,1)S(1)} async-done(((bf16[32,8,512]{2,0,1:T(8,128)(2,1)}), bf16[32,8,512]{2,0,1:T(8,128)(2,1)S(1)}, u32[]{:S(2)}, u32[]{:S(2)}) %all-to-all-start) | async-done | bytes 262176 | tf_op jit(solution)/shard_map/all_to_all | solution.py:38
  24.0 0.6 copy-done.2
  24.6 0.3 fusion.12
  24.9 0.8 %pad_maximum_fusion = f32[8,128,128]{2,1,0:T(8,128)} fusion(f32[4,128,128]{2,1,0:T(8,128)S(1)} %fusion.12, f32[4,128,128]{2,1,0:T(8,128)S(1)} %fusion.7), kind=kLoop, calls=%fused_computation.9 | loop fusion | flops 131072 | bytes 1048576 | tf_op jit(solution)/shard_map/concatenate | solution.py:45
  25.8 12.5 %all-to-all-start.1 = ((f32[64,16,128]{2,1,0:T(8,128)}), f32[64,16,128]{2,1,0:T(8,128)S(1)}, u32[]{:S(2)}, u32[]{:S(2)}) async-start(f32[64,16,128]{2,1,0:T(8,128)} %bitcast.11), calls=%async_computation.1 | async-start | bytes 1048576 | tf_op jit(solution)/shard_map/all_to_all | solution.py:46
  38.2 0.7 copy-done.6
  39.1 0.3 fusion
  39.4 16.1 %all-to-all-done.1 = f32[64,16,128]{2,1,0:T(8,128)S(1)} async-done(((f32[64,16,128]{2,1,0:T(8,128)}), f32[64,16,128]{2,1,0:T(8,128)S(1)}, u32[]{:S(2)}, u32[]{:S(2)}) %all-to-all-start.1) | async-done | bytes 524320 | tf_op jit(solution)/shard_map/all_to_all | solution.py:46
  55.5 0.6 convolution_convert_fusion
  56.1 0.9 %copy.53 = bf16[64,16,128]{2,1,0:T(8,128)(2,1)} copy(bf16[64,16,128]{2,0,1:T(8,128)(2,1)S(1)} %convolution_convert_fusion) | data formatting | bytes 524288 | tf_op jit(solution)/shard_map/convert_element_type | solution.py:54
  56.9 6.3 %all-to-all-start.2 = ((bf16[64,16,128]{2,1,0:T(8,128)(2,1)}), bf16[64,16,128]{2,1,0:T(8,128)(2,1)S(1)}, u32[]{:S(2)}, u32[]{:S(2)}) async-start(bf16[64,16,128]{2,1,0:T(8,128)(2,1)} %copy.53), calls=%async_computation.2 | async-start | bytes 524288 | tf_op jit(solution)/shard_map/all_to_all | solution.py:54
  63.2 1.0 %convolution_convert_fusion.2.refs_0_ = bf16[4,256,128]{2,1,0:T(8,128)(2,1)} fusion(bf16[4,256,256]{2,1,0:T(8,128)(2,1)S(1)} %fusion, bf16[4,128,256]{1,2,0:T(8,128)(2,1)S(1)} %get-tuple-element.4), kind=kOutput, calls=%fused_computation.8 | convolution fusion | flops 67239936 | bytes 1048576 | tf_op jit(solution)/shard_map/hts,hds->htd/dot_general | solution.py:112
  64.2 1.0 %convolution_convert_fusion.1.refs_1_ = bf16[4,256,128]{2,1,0:T(8,128)(2,1)} fusion(bf16[4,256,256]{2,1,0:T(8,128)(2,1)S(1)} %fusion, bf16[4,128,256]{1,2,0:T(8,128)(2,1)S(1)} %get-tuple-element.3), kind=kOutput, calls=%fused_computation.7 | convolution fusion | flops 67239936 | bytes 1048576 | tf_op jit(solution)/shard_map/hts,hdt->hsd/dot_general | solution.py:113
  65.3 1.3 %fusion.3.refs_2_ = bf16[4,256,128]{2,1,0:T(8,128)(2,1)} fusion(bf16[4,128,256]{1,2,0:T(8,128)(2,1)S(1)} %get-tuple-element.3, bf16[4,128,256]{1,2,0:T(8,128)(2,1)S(1)} %get-tuple-element.4, f32[256,256]{1,0:T(8,128)S(1)} %fusion.6, bf16[256,4,128]{2,1,0:T(4,128)(2,1)S(1)} %reshape_reshape.3), kind=kOutput, calls=%fused_computation.5 | convolution fusion | flops 134873088 | bytes 1310720 | tf_op jit(solution)/shard_map/hts,the->hse/dot_general | solution.py:114
  66.5 8.7 %all-to-all-done.2 = bf16[64,16,128]{2,1,0:T(8,128)(2,1)S(1)} async-done(((bf16[64,16,128]{2,1,0:T(8,128)(2,1)}), bf16[64,16,128]{2,1,0:T(8,128)(2,1)S(1)}, u32[]{:S(2)}, u32[]{:S(2)}) %all-to-all-start.2) | async-done | bytes 262176 | tf_op jit(solution)/shard_map/all_to_all | solution.py:54
  75.2 0.7 copy-done.3
  75.9 2.6 %finish_outputs.1 = (bf16[256,512]{1,0:T(8,128)(2,1)}, bf16[256,512]{1,0:T(8,128)(2,1)}, bf16[256,512]{1,0:T(8,128)(2,1)}) custom-call(bf16[4,256,128]{2,1,0:T(8,128)(2,1)} %convolution_convert_fusion.2.refs_0_, bf16[4,256,128]{2,1,0:T(8,128)(2,1)} %convolution_convert_fusion.1.refs_1_, bf16[4,256,128]{2,1,0:T(8,128)(2,1)} %fusion.3.refs_2_, ...), custom_call_target="tpu_custom_call" | custom-call | flops 100663296 | bytes 2359296 | tf_op jit(solution)/shard_map/finish_outputs/pallas_call | solution.py:79
  (19 shorter events, 0.7 us)
Async XLA Ops:
  2.4 11.0 %copy-start.4 = (s32[32,256]{1,0:T(8,128)S(1)}, s32[32,256]{1,0:T(8,128)}, u32[]{:S(2)}) copy-start(s32[32,256]{1,0:T(8,128)} %param.6) | copy-start | bytes 98308
  2.5 21.5 %all-to-all-start = ((bf16[32,8,512]{2,0,1:T(8,128)(2,1)}), bf16[32,8,512]{2,0,1:T(8,128)(2,1)S(1)}, u32[]{:S(2)}, u32[]{:S(2)}) async-start(bf16[32,8,512]{2,0,1:T(8,128)(2,1)} %copy.37), calls=%async_computation | async-start | bytes 524288 | tf_op jit(solution)/shard_map/all_to_all | solution.py:38
  13.5 0.8 copy-start.5
  14.6 1.0 %copy-start.1 = (bf16[256,512]{1,0:T(8,128)(2,1)S(1)}, bf16[256,512]{1,0:T(8,128)(2,1)}, u32[]{:S(2)}) copy-start(bf16[256,512]{1,0:T(8,128)(2,1)} %refs_4_.1) | copy-start | bytes 786436
  14.7 50.5 %copy-start = (bf16[4,128,256]{1,2,0:T(8,128)(2,1)}, bf16[4,128,256]{1,2,0:T(8,128)(2,1)S(1)}, u32[]{:S(2)}) copy-start(bf16[4,128,256]{1,2,0:T(8,128)(2,1)S(1)} %get-tuple-element.4) | copy-start | bytes 786436
  23.9 0.7 copy-start.2
  25.8 29.7 %all-to-all-start.1 = ((f32[64,16,128]{2,1,0:T(8,128)}), f32[64,16,128]{2,1,0:T(8,128)S(1)}, u32[]{:S(2)}, u32[]{:S(2)}) async-start(f32[64,16,128]{2,1,0:T(8,128)} %bitcast.11), calls=%async_computation.1 | async-start | bytes 1048576 | tf_op jit(solution)/shard_map/all_to_all | solution.py:46
  38.2 0.7 copy-start.6
  56.9 18.3 %all-to-all-start.2 = ((bf16[64,16,128]{2,1,0:T(8,128)(2,1)}), bf16[64,16,128]{2,1,0:T(8,128)(2,1)S(1)}, u32[]{:S(2)}, u32[]{:S(2)}) async-start(bf16[64,16,128]{2,1,0:T(8,128)(2,1)} %copy.53), calls=%async_computation.2 | async-start | bytes 524288 | tf_op jit(solution)/shard_map/all_to_all | solution.py:54
  75.2 0.7 copy-start.3

commit v10 on v0

--- a/solution.py
+++ b/solution.py
@@ -47,7 +47,7 @@
     col = jnp.arange(n_ctx, dtype=jnp.int32)[None, :]
     mix = jnp.where(me < n_ctx // 2, col < row, col > row).astype(f32)
     sums = jnp.dot(
-        mix, got.reshape(n_ctx, -1), precision=lax.Precision.HIGHEST, preferred_element_type=f32
+        mix, got.reshape(n_ctx, -1), precision=lax.Precision.HIGH, preferred_element_type=f32
     )
     back = lax.all_to_all(sums.astype(jnp.bfloat16).reshape(n_ctx, -1, HD), CTX, 0, 0, tiled=True)
     both = back.reshape(2, heads, HD, HD)

time: 78.9 us -> 78.8 us (level)
  no operation moved by 1% of the time
where the time goes in v10:
time: 78.8 us; the launch traced here: 78.3 us
  waiting for transfers between devices  37.5 us (48%)
  starting transfers between devices  29.7 us (38%)
  local copies, waits for them, and re-layouts  6.3 us (8%)
  matrix products  2.99 us (4%)
  other arithmetic  1.06 us (1%)
  between operations  0.8 us (1%)
    all_to_all x1, waiting for transfers between devices, carried_sums(): got = lax.all_to_all(terms, CTX, 0, 0, tiled=True)  16.4 us
    all_to_all x1, starting transfers between devices, carried_sums(): got = lax.all_to_all(terms, CTX, 0, 0, tiled=True)  12.4 us
    all_to_all x1, waiting for transfers between devices, carried_sums(): lax.all_to_all(sums.astype(jnp.bfloat16).reshape(n_ctx, -1, HD), CTX, 0,...  11.1 us
    all_to_all x1, starting transfers between devices, gather_heads(): got = lax.all_to_all(blocks, 'head', 0, 0, tiled=True)  11 us
    all_to_all x1, waiting for transfers between devices, gather_heads(): got = lax.all_to_all(blocks, 'head', 0, 0, tiled=True)  9.98 us
    all_to_all x1, starting transfers between devices, carried_sums(): lax.all_to_all(sums.astype(jnp.bfloat16).reshape(n_ctx, -1, HD), CTX, 0,...  6.29 us
    unnamed x13, local copies, waits for them, and re-layouts  5.04 us
  transfers between devices with their start and end apart: 3, of which 3 were waited for; matrix products, arithmetic and copies ran while one was open for 2% of the time, Pallas kernels for 0%

profile of v10, /device:TPU:1, one launch (start us, length us, event | category | flops | bytes accessed | tf_op | source)
XLA Modules:
  0.0 78.3 jit_solution(5513512044171173917)
XLA Ops:
  0.6 1.1 %copy.30 = bf16[4,8,8,512]{3,2,1,0:T(8,128)(2,1)S(1)} copy(bf16[4,8,8,512]{3,1,2,0:T(8,128)(2,1)} %bitcast.95) | data formatting | bytes 524288
  1.7 0.8 copy.52
  2.5 11.0 %all-to-all-start = ((bf16[8,32,512]{2,1,0:T(8,128)(2,1)}), bf16[8,32,512]{2,1,0:T(8,128)(2,1)S(1)}, u32[]{:S(2)}, u32[]{:S(2)}) async-start(bf16[8,32,512]{2,1,0:T(8,128)(2,1)} %bitcast.85), calls=%async_computation | async-start | bytes 524288 | tf_op jit(solution)/shard_map/all_to_all | solution.py:36
  13.8 0.2 fusion.19
  14.0 10.0 %all-to-all-done = bf16[8,32,512]{2,1,0:T(8,128)(2,1)S(1)} async-done(((bf16[8,32,512]{2,1,0:T(8,128)(2,1)}), bf16[8,32,512]{2,1,0:T(8,128)(2,1)S(1)}, u32[]{:S(2)}, u32[]{:S(2)}) %all-to-all-start) | async-done | bytes 262176 | tf_op jit(solution)/shard_map/all_to_all | solution.py:36
  24.2 0.2 fusion.30
  24.5 0.8 %pad_maximum_fusion = f32[8,128,128]{2,1,0:T(8,128)} fusion(f32[4,128,128]{2,1,0:T(8,128)S(1)} %fusion.30, f32[4,128,128]{2,1,0:T(8,128)S(1)} %fusion.19), kind=kLoop, calls=%fused_computation.19 | loop fusion | flops 131072 | bytes 1048576 | tf_op jit(solution)/shard_map/concatenate | solution.py:43
  25.3 12.4 %all-to-all-start.1 = ((f32[64,16,128]{2,1,0:T(8,128)}), f32[64,16,128]{2,1,0:T(8,128)S(1)}, u32[]{:S(2)}, u32[]{:S(2)}) async-start(f32[64,16,128]{2,1,0:T(8,128)} %bitcast.6), calls=%async_computation.1 | async-start | bytes 1048576 | tf_op jit(solution)/shard_map/all_to_all | solution.py:44
  37.8 0.7 copy-done.3
  38.6 16.4 %all-to-all-done.1 = f32[64,16,128]{2,1,0:T(8,128)S(1)} async-done(((f32[64,16,128]{2,1,0:T(8,128)}), f32[64,16,128]{2,1,0:T(8,128)S(1)}, u32[]{:S(2)}, u32[]{:S(2)}) %all-to-all-start.1) | async-done | bytes 524320 | tf_op jit(solution)/shard_map/all_to_all | solution.py:44
  55.1 0.4 fusion.9
  55.5 0.7 copy.33
  56.2 6.3 %all-to-all-start.2 = ((bf16[64,16,128]{2,1,0:T(8,128)(2,1)}), bf16[64,16,128]{2,1,0:T(8,128)(2,1)S(1)}, u32[]{:S(2)}, u32[]{:S(2)}) async-start(bf16[64,16,128]{2,1,0:T(8,128)(2,1)} %bitcast.29), calls=%async_computation.2 | async-start | bytes 524288 | tf_op jit(solution)/shard_map/all_to_all | solution.py:52
  62.5 0.3 fusion
  62.9 0.3 fusion.29
  63.2 0.2 fusion.31
  63.4 11.1 %all-to-all-done.2 = bf16[64,16,128]{2,1,0:T(8,128)(2,1)S(1)} async-done(((bf16[64,16,128]{2,1,0:T(8,128)(2,1)}), bf16[64,16,128]{2,1,0:T(8,128)(2,1)S(1)}, u32[]{:S(2)}, u32[]{:S(2)}) %all-to-all-start.2) | async-done | bytes 262176 | tf_op jit(solution)/shard_map/all_to_all | solution.py:52
  74.5 0.3 fusion.3
  74.8 0.5 fusion.8
  75.3 0.8 %copy.27 = bf16[256,512]{1,0:T(8,128)(2,1)} copy(bf16[256,512]{0,1:T(8,128)(2,1)S(1)} %bitcast.89) | data formatting | bytes 524288
  76.2 0.2 fusion.6
  76.4 0.8 %copy.25 = bf16[256,512]{1,0:T(8,128)(2,1)} copy(bf16[256,512]{0,1:T(8,128)(2,1)S(1)} %bitcast.92) | data formatting | bytes 524288
  77.3 0.2 fusion.7
  77.5 0.8 %copy.26 = bf16[256,512]{1,0:T(8,128)(2,1)} copy(bf16[256,512]{0,1:T(8,128)(2,1)S(1)} %bitcast.93) | data formatting | bytes 524288
  (16 shorter events, 0.7 us)
Async XLA Ops:
  0.6 13.2 %copy-start = (bf16[256,512]{1,0:T(8,128)(2,1)S(1)}, bf16[256,512]{1,0:T(8,128)(2,1)}, u32[]{:S(2)}) copy-start(bf16[256,512]{1,0:T(8,128)(2,1)} %param.7) | copy-start | bytes 786436
  2.5 11.1 %copy-start.1 = (s32[32,256]{1,0:T(8,128)S(1)}, s32[32,256]{1,0:T(8,128)}, u32[]{:S(2)}) copy-start(s32[32,256]{1,0:T(8,128)} %param.5) | copy-start | bytes 98308
  2.5 11.1 %copy-start.2 = (s32[32,256]{1,0:T(8,128)S(1)}, s32[32,256]{1,0:T(8,128)}, u32[]{:S(2)}) copy-start(s32[32,256]{1,0:T(8,128)} %param.6) | copy-start | bytes 98308
  2.5 21.5 %all-to-all-start = ((bf16[8,32,512]{2,1,0:T(8,128)(2,1)}), bf16[8,32,512]{2,1,0:T(8,128)(2,1)S(1)}, u32[]{:S(2)}, u32[]{:S(2)}) async-start(bf16[8,32,512]{2,1,0:T(8,128)(2,1)} %bitcast.85), calls=%async_computation | async-start | bytes 524288 | tf_op jit(solution)/shard_map/all_to_all | solution.py:36
  25.3 29.7 %all-to-all-start.1 = ((f32[64,16,128]{2,1,0:T(8,128)}), f32[64,16,128]{2,1,0:T(8,128)S(1)}, u32[]{:S(2)}, u32[]{:S(2)}) async-start(f32[64,16,128]{2,1,0:T(8,128)} %bitcast.6), calls=%async_computation.1 | async-start | bytes 1048576 | tf_op jit(solution)/shard_map/all_to_all | solution.py:44
  37.8 0.7 copy-start.3
  56.2 18.3 %all-to-all-start.2 = ((bf16[64,16,128]{2,1,0:T(8,128)(2,1)}), bf16[64,16,128]{2,1,0:T(8,128)(2,1)S(1)}, u32[]{:S(2)}, u32[]{:S(2)}) async-start(bf16[64,16,128]{2,1,0:T(8,128)(2,1)} %bitcast.29), calls=%async_computation.2 | async-start | bytes 524288 | tf_op jit(solution)/shard_map/all_to_all | solution.py:52
